TPU v7x, 32 devices: a whole 2x2x4 slice. The times are simulated.
32 devices in a mesh: freq: 4 (over y, x), rblk: 8 (over z, core).
Axes of the slice: x: 2, y: 2, z: 4, core: 2. Of those that a mesh axis runs over, the one named last changes fastest.
Arguments:
- response: bfloat16 [8, 2, 64, 49, 128, 128], P('freq', None, 'rblk'), as said below
- aperture: int32 [64, 49], replicated, may hold values from -1 to 63, as said below
- focus_init: bfloat16 [8, 2, 4, 8192], P('freq', None, None, 'rblk'), may hold values from -6 to 6
- arrival: int32 [4, 8192], P(None, 'rblk'), may hold values from 512 to 3583
Outputs:
- focus_plus: bfloat16 [8, 2, 4, 8192], P('freq', None, None, 'rblk')
- focus_minus: bfloat16 [8, 2, 4, 8192], P('freq', None, None, 'rblk')
Inputs may be any that keep to these rules, and one draw needn't show every extreme that they name: `aperture`: row b lists, in rising order, the source blocks that receiver block b needs, then -1 in its other slots. Blocks lie on a 8 x 8 grid: block b sits in grid row 2 * ((b % h) // 8) + b // h and grid column b % 8, with h half of 64. A block lists itself and only blocks at most 3 apart along each grid direction; b lists c exactly when c lists b; some block lists 49 blocks. response[:, :, b, j] is the block of R for receivers of block b and sources of block aperture[b, j]; slots with -1 hold values that are not part of R. Reciprocity: that block is the transpose of the block stored for receivers of block aperture[b, j] and sources of block b.
All inputs are finite; a program needn't handle non-finite values.
Results may differ from a plain program's by a relative error of at most 0.005.
Values may be sent and summed in bfloat16 or wider, within the bound.
No kernel may reach another device: no remote copies, remote signals or barrier semaphores. Data moves between devices by JAX's collectives and lax.ppermute only.
A program may use at most 192 MiB of HBM per device.

v0:
```python
import math

import jax
import jax.numpy as jnp
from jax import lax
from jax.experimental import pallas as pl
from jax.experimental.pallas import tpu as pltpu
from jax.sharding import PartitionSpec as P

NT = 4096
FBASE = 256
ITERS = 1
NBUF = 3


def chunk_width(aper_w):
    for width in range(min(8, aper_w), 0, -1):
        if aper_w % width == 0:
            return width
    return 1


def chunk_schedule(aperture, first_block, blk_dev, chunk):
    aper_w = aperture.shape[1]
    per_blk = aper_w // chunk
    rows = lax.dynamic_slice_in_dim(aperture, first_block, blk_dev, 0)
    live = jnp.sum((rows >= 0).astype(jnp.int32), axis=1)
    counts = (live + chunk - 1) // chunk
    ends = jnp.cumsum(counts)
    starts = ends - counts
    entry = jnp.arange(blk_dev * per_blk, dtype=jnp.int32)
    blocks = jnp.sum((ends[None, :] <= entry[:, None]).astype(jnp.int32), axis=1)
    blocks = jnp.minimum(blocks, blk_dev - 1)
    chunks = jnp.clip(entry - starts[blocks], 0, per_blk - 1)
    meta = jnp.stack([first_block.astype(jnp.int32), ends[-1]])
    return blocks, chunks, meta, live


def block_products(gathered, response, aperture, first_block, conjugate):
    freq_dev, unused, blk_dev, aper_w, block_rows, block_cols = response.shape
    rows_g = gathered.shape[2]
    chunk = chunk_width(aper_w)
    blocks, chunks, meta, live = chunk_schedule(aperture, first_block, blk_dev, chunk)
    flat_aperture = aperture.reshape(-1)
    focal = rows_g // 2

    def kernel(aper_ref, blk_ref, chk_ref, meta_ref, live_ref, resp_hbm, g_ref, out_ref,
               buf, sem, acc):
        first = meta_ref[0]
        total = meta_ref[1]
        acc[...] = jnp.zeros(acc.shape, jnp.float32)

        def start(entry, slot):
            b = blk_ref[entry]
            c = chk_ref[entry]
            pltpu.make_async_copy(
                resp_hbm.at[:, :, b, pl.ds(c * chunk, chunk)], buf.at[slot], sem.at[slot]
            ).start()

        for slot in range(NBUF):
            @pl.when(slot < total)
            def _():
                start(slot, slot)

        def body(entry, carry):
            slot = entry % NBUF
            b = blk_ref[entry]
            c = chk_ref[entry]
            pltpu.make_async_copy(
                resp_hbm.at[:, :, 0, pl.ds(0, chunk)], buf.at[slot], sem.at[slot]
            ).wait()
            count = live_ref[b]
            row = first + b
            for t in range(chunk):
                j = c * chunk + t

                @pl.when(j < count)
                def _():
                    src = aper_ref[row * aper_w + j]
                    for f in range(freq_dev):
                        piece = g_ref[src, f]
                        tile = buf[slot, f, :, t].reshape(2 * block_rows, block_cols)
                        acc[b, f] += lax.dot_general(
                            piece, tile, (((1,), (1,)), ((), ())),
                            preferred_element_type=jnp.float32,
                        )

            @pl.when(entry + NBUF < total)
            def _():
                start(entry + NBUF, slot)

            return carry

        lax.fori_loop(0, total, body, 0)

        for b in range(blk_dev):
            for f in range(freq_dev):
                v = acc[b, f]
                p00 = v[0:focal, 0:block_rows]
                p01 = v[0:focal, block_rows:]
                p10 = v[focal:, 0:block_rows]
                p11 = v[focal:, block_rows:]
                if conjugate:
                    real_part = p00 + p11
                    imag_part = p10 - p01
                else:
                    real_part = p00 - p11
                    imag_part = p10 + p01
                cols = pl.ds(b * block_rows, block_rows)
                out_ref[f, 0, :, cols] = real_part.astype(out_ref.dtype)
                out_ref[f, 1, :, cols] = imag_part.astype(out_ref.dtype)

    smem = pl.BlockSpec(memory_space=pltpu.SMEM)
    vmem = pl.BlockSpec(memory_space=pltpu.VMEM)
    return pl.pallas_call(
        kernel,
        out_shape=jax.ShapeDtypeStruct(
            (freq_dev, 2, focal, blk_dev * block_rows), jnp.bfloat16
        ),
        in_specs=[smem, smem, smem, smem, smem, pl.BlockSpec(memory_space=pl.ANY), vmem],
        out_specs=vmem,
        scratch_shapes=[
            pltpu.VMEM((NBUF, freq_dev, 2, chunk, block_rows, block_cols), response.dtype),
            pltpu.SemaphoreType.DMA((NBUF,)),
            pltpu.VMEM((blk_dev, freq_dev, rows_g, 2 * block_rows), jnp.float32),
        ],
    )(flat_aperture, blocks, chunks, meta, live, response, gathered)


def gather_columns(spectra, block_rows):
    freq_dev, unused, focal, traces = spectra.shape
    blk_dev = traces // block_rows
    local = spectra.reshape(freq_dev, 2 * focal, blk_dev, block_rows)
    local = jnp.transpose(local, (2, 0, 1, 3))
    return lax.all_gather(local, "rblk", axis=0, tiled=True)


def dirichlet(offsets, limits):
    span = 2 * NT
    full_turn = (limits * offsets) % span
    half_turn = ((limits - 1) * offsets) % span
    base_turn = offsets % span
    is_zero = (offsets % NT) == 0
    denom = jnp.where(
        is_zero, jnp.float32(1.0), jnp.sin(jnp.float32(math.pi) * base_turn.astype(jnp.float32) / NT)
    )
    ratio = jnp.where(
        is_zero,
        limits.astype(jnp.float32),
        jnp.sin(jnp.float32(math.pi) * full_turn.astype(jnp.float32) / NT) / denom,
    )
    angle = jnp.float32(math.pi) * half_turn.astype(jnp.float32) / NT
    return ratio * jnp.cos(angle), ratio * jnp.sin(angle)


def window_tables(arrival, freq_dev, freq_all):
    first = lax.axis_index("freq") * freq_dev
    mine = FBASE + first + jnp.arange(freq_dev, dtype=jnp.int32)
    every = FBASE + jnp.arange(freq_all, dtype=jnp.int32)
    limits = arrival[None, None]
    near_re, near_im = dirichlet((mine[:, None] - every[None, :])[:, :, None, None], limits)
    far_re, far_im = dirichlet((-(mine[:, None] + every[None, :]))[:, :, None, None], limits)
    scale = jnp.float32(1.0 / NT)
    return (
        (near_re + far_re) * scale,
        (far_im - near_im) * scale,
        (near_im + far_im) * scale,
        (near_re - far_re) * scale,
    )


def apply_window(spectra, tables):
    c_rr, c_ir, c_ri, c_ii = tables
    values = spectra.astype(jnp.float32)
    real_in = values[:, 0][:, None]
    imag_in = values[:, 1][:, None]
    new_real = jnp.sum(real_in * c_rr + imag_in * c_ir, axis=0)
    new_imag = jnp.sum(real_in * c_ri + imag_in * c_ii, axis=0)
    partial = jnp.stack([new_real, new_imag], axis=1)
    summed = lax.psum_scatter(partial, "freq", scatter_dimension=0, tiled=True)
    return summed.astype(jnp.bfloat16)


def shards(response, aperture, focus_init, arrival):
    freq_dev = response.shape[0]
    blk_dev = response.shape[2]
    block_rows = response.shape[4]
    freq_all = freq_dev * lax.axis_size("freq")
    first_block = lax.axis_index("rblk") * blk_dev
    tables = window_tables(arrival, freq_dev, freq_all)
    current = focus_init
    window_q = focus_init
    for iteration in range(ITERS):
        gathered = gather_columns(current, block_rows)
        forward = block_products(gathered, response, aperture, first_block, False)
        window_q = apply_window(forward, tables)
        mirrored = gather_columns(window_q, block_rows)
        adjoint = block_products(mirrored, response, aperture, first_block, True)
        windowed = apply_window(adjoint, tables)
        current = (focus_init.astype(jnp.float32) + windowed.astype(jnp.float32)).astype(
            jnp.bfloat16
        )
    return (current, window_q)


def solution(mesh):
    return jax.shard_map(
        shards,
        mesh=mesh,
        in_specs=(
            P("freq", None, "rblk", None, None, None),
            P(),
            P("freq", None, None, "rblk"),
            P(None, "rblk"),
        ),
        out_specs=(P("freq", None, None, "rblk"), P("freq", None, None, "rblk")),
        check_vma=False,
    )
```

profile of v0, /device:TPU:8, one launch (start us, length us, event | category | flops | bytes accessed | tf_op | source)
XLA Modules:
  0.0 152.1 jit_solution(14137563352625474814)
XLA Ops:
  0.6 0.0 copy-start.4
  0.6 0.0 copy-start.2
  0.7 0.8 convert_reduce_fusion.live_ref
  1.5 0.2 reduce-window.4
  1.7 0.7 fusion.33
  2.4 0.1 convert_reduce_fusion.1
  2.5 5.5 %fusion.31 = (s32[56]{0:T(128)}, s32[56]{0:T(128)}) fusion(s32[]{:T(128)} %bitcast.6, s32[]{:T(128)} %bitcast.7, s32[]{:T(128)} %bitcast.8, s32[]{:T(128)} %bitcast.9, s32[]{:T(128)} %bitcast.10, s32[]{:T(128)} %bitcast.12, s32[]{:T(128)} %bitcast.11, s32[]{:T(128)} %bitcast.5, s32[56]{0:T(128)S(1)} %convert_reduce_fusion.1), kind=kLoop, calls=%fused_computation.99 | loop fusion | flops 1120 | bytes 704 | tf_op jit(solution)/shard_map/jit(clip)/min | solution.py:34
  8.0 0.6 slice.19
  8.6 1.3 pad_add_fusion.meta_ref
  9.9 0.8 copy.12
  10.7 0.7 reshape.348.aper_ref
  11.5 0.8 reshape.349
  12.3 15.5 %all_gather.6.g_ref = bf16[64,2,8,128]{3,2,1,0:T(8,128)(2,1)} all-gather(bf16[8,2,8,128]{3,2,1,0:T(8,128)(2,1)S(1)} %copy.13), channel_id=1, replica_groups=mesh['freq'=4,'rblk'=8] {'rblk'}, dimensions={0}, use_global_device_ids=true | all-gather | bytes 294912 | tf_op jit(solution)/shard_map/all_gather | solution.py:135
  27.8 0.0 copy-done.3
  27.8 30.0 %shard_map.59 = bf16[2,2,4,1024]{3,2,1,0:T(4,128)(2,1)} custom-call(s32[3136]{0:T(1024)} %reshape.348.aper_ref, s32[56]{0:T(128)} %get-tuple-element.21.blk_ref, s32[56]{0:T(128)} %get-tuple-element.20.chk_ref, s32[2]{0:T(128)} %pad_add_fusion.meta_ref, s32[8]{0:T(128)} %copy-done.3, bf16[2,2,8,49,128,128]{5,4,3,2,1,0:T(8,128)(2,1)} %resp_hbm.3, ...), custom_call_target="tpu_custom_call" | custom-call | tf_op jit(solution)/shard_map/pallas_call | solution.py:115
  57.8 0.8 convert_element_type.72
  58.6 0.1 add_negate_fusion
  58.7 0.1 sine_select_fusion
  58.8 0.1 fusion.27
  58.9 4.2 %add_reduce_fusion.3 = (f32[8,4,1024]{2,0,1:T(8,128)S(1)}, f32[8,4,1024]{2,0,1:T(8,128)S(1)}) fusion(f32[2,4,1024]{2,1,0:T(4,128)S(1)} %get-tuple-element.11, f32[2,4,1024]{2,1,0:T(4,128)S(1)} %get-tuple-element.10, f32[2,8]{1,0:T(2,128)S(1)} %get-tuple-element.19, s32[2,8]{1,0:T(2,128)S(1)} %get-tuple-element.17, pred[2,8]{1,0:T(4,128)(4,1)S(1)} %get-tuple-element.15, ...), kind=kLoop, calls=%fused_computation.43 | loop fusion | flops 4915200 | bytes 377120 | tf_op jit(solution)/shard_map/reduce_sum | solution.py:177
  63.1 0.2 copy.14
  63.3 20.3 %all-reduce.4 = bf16[8,2,4,1024]{3,2,1,0:T(4,128)(2,1)S(1)} all-reduce(f32[8,2,4,1024]{3,2,1,0:T(4,128)S(1)} %copy.14), channel_id=2, replica_groups=mesh['freq'=4,'rblk'=8] {'freq'}, use_global_device_ids=true, to_apply=%region_5.6.clone | all-reduce | flops 65536 | bytes 393216
  83.6 0.0 copy-done.4
  83.6 0.6 dynamic-slice
  84.8 0.0 copy-start.1
  84.9 13.6 %all_gather.7.g_ref = bf16[64,2,8,128]{3,2,1,0:T(8,128)(2,1)} all-gather(bf16[8,2,8,128]{3,2,1,0:T(8,128)(2,1)S(1)} %copy.15), channel_id=1, replica_groups=mesh['freq'=4,'rblk'=8] {'rblk'}, dimensions={0}, use_global_device_ids=true | all-gather | bytes 294912 | tf_op jit(solution)/shard_map/all_gather | solution.py:135
  98.5 29.9 %shard_map.60 = bf16[2,2,4,1024]{3,2,1,0:T(4,128)(2,1)} custom-call(s32[3136]{0:T(1024)} %reshape.348.aper_ref, s32[56]{0:T(128)} %get-tuple-element.21.blk_ref, s32[56]{0:T(128)} %get-tuple-element.20.chk_ref, s32[2]{0:T(128)} %pad_add_fusion.meta_ref, s32[8]{0:T(128)} %copy-done.3, bf16[2,2,8,49,128,128]{5,4,3,2,1,0:T(8,128)(2,1)} %resp_hbm.3, ...), custom_call_target="tpu_custom_call" | custom-call | tf_op jit(solution)/shard_map/pallas_call | solution.py:115
  128.4 0.8 convert_element_type.74
  129.2 4.2 %add_reduce_fusion.1 = (f32[8,4,1024]{2,0,1:T(8,128)S(1)}, f32[8,4,1024]{2,0,1:T(8,128)S(1)}) fusion(f32[2,4,1024]{2,1,0:T(4,128)S(1)} %get-tuple-element.9, f32[2,4,1024]{2,1,0:T(4,128)S(1)} %get-tuple-element.8, f32[2,8]{1,0:T(2,128)S(1)} %get-tuple-element.19, s32[2,8]{1,0:T(2,128)S(1)} %get-tuple-element.17, pred[2,8]{1,0:T(4,128)(4,1)S(1)} %get-tuple-element.15, ...), kind=kLoop, calls=%fused_computation.41 | loop fusion | flops 4915200 | bytes 377120 | tf_op jit(solution)/shard_map/reduce_sum | solution.py:177
  133.4 0.2 copy.16
  133.6 17.9 %all-reduce.5 = bf16[8,2,4,1024]{3,2,1,0:T(4,128)(2,1)S(1)} all-reduce(f32[8,2,4,1024]{3,2,1,0:T(4,128)S(1)} %copy.16), channel_id=3, replica_groups=mesh['freq'=4,'rblk'=8] {'freq'}, use_global_device_ids=true, to_apply=%region_8.9.clone | all-reduce | flops 65536 | bytes 393216
  151.5 0.6 add_convert_fusion
  (18 shorter events, 0.2 us)
Async XLA Ops:
  0.6 82.9 %copy-start.4 = (u32[32]{0:T(128)S(1)}, u32[32]{0:T(128)}, u32[]{:S(2)}) copy-start(u32[32]{0:T(128)} %constant.142) | copy-start | bytes 388
  0.6 58.2 %copy-start.2 = (s32[4,1024]{1,0:T(4,128)S(1)}, s32[4,1024]{1,0:T(4,128)}, u32[]{:S(2)}) copy-start(s32[4,1024]{1,0:T(4,128)} %param.7) | copy-start | bytes 49156
  1.5 26.3 %copy-start.3 = (s32[8]{0:T(128)}, s32[8]{0:T(128)S(1)}, u32[]{:S(2)}) copy-start(s32[8]{0:T(128)S(1)} %convert_reduce_fusion.live_ref) | copy-start | bytes 100
  27.8 123.7 %copy-start = (bf16[2,2,4,1024]{3,2,1,0:T(4,128)(2,1)S(1)}, bf16[2,2,4,1024]{3,2,1,0:T(4,128)(2,1)}, u32[]{:S(2)}) copy-start(bf16[2,2,4,1024]{3,2,1,0:T(4,128)(2,1)} %param.6) | copy-start | bytes 98308
  84.8 67.3 %copy-start.1 = (bf16[2,2,4,1024]{3,2,1,0:T(4,128)(2,1)}, bf16[2,2,4,1024]{3,2,1,0:T(4,128)(2,1)S(1)}, u32[]{:S(2)}) copy-start(bf16[2,2,4,1024]{3,2,1,0:T(4,128)(2,1)S(1)} %dynamic-slice_convert_fusion.1) | copy-start | bytes 98308
where the time goes:
time: 153 us; the launch traced here: 152 us
  blocking collectives  67.2 us (44%)
  Pallas kernels  59.9 us (39%)
  other arithmetic  18.9 us (12%)
  local copies, waits for them, and re-layouts  4.6 us (3%)
    pallas_call x2, Pallas kernels, block_products(): pl.pallas_call(kernel, out_shape=jax.ShapeDtypeStruct((freq_dev, 2, focal...  59.9 us
    unnamed x2, blocking collectives  38.1 us
    all_gather x2, blocking collectives, gather_columns(): return lax.all_gather(local, 'rblk', axis=0, tiled=True)  29.1 us
    reduce_sum x2, other arithmetic, apply_window(): new_real = jnp.sum(real_in * c_rr + imag_in * c_ir, axis=0)  8.35 us
    min x1, other arithmetic, chunk_schedule(): chunks = jnp.clip(entry - starts[blocks], 0, per_blk - 1)  5.53 us

commit v1 on v0

--- a/solution.py
+++ b/solution.py
@@ -38,56 +38,60 @@
 
 def block_products(gathered, response, aperture, first_block, conjugate):
     freq_dev, unused, blk_dev, aper_w, block_rows, block_cols = response.shape
-    rows_g = gathered.shape[2]
+    rows_g = gathered.shape[3]
     chunk = chunk_width(aper_w)
     blocks, chunks, meta, live = chunk_schedule(aperture, first_block, blk_dev, chunk)
     flat_aperture = aperture.reshape(-1)
     focal = rows_g // 2
 
     def kernel(aper_ref, blk_ref, chk_ref, meta_ref, live_ref, resp_hbm, g_ref, out_ref,
-               buf, sem, acc):
+               buf, sem, pcat, acc):
         first = meta_ref[0]
         total = meta_ref[1]
         acc[...] = jnp.zeros(acc.shape, jnp.float32)
 
-        def start(entry, slot):
+        def copies(entry, slot):
             b = blk_ref[entry]
             c = chk_ref[entry]
-            pltpu.make_async_copy(
-                resp_hbm.at[:, :, b, pl.ds(c * chunk, chunk)], buf.at[slot], sem.at[slot]
-            ).start()
+            return [
+                pltpu.make_async_copy(
+                    resp_hbm.at[:, :, b, c * chunk + t],
+                    buf.at[slot, :, :, :, pl.ds(t * block_cols, block_cols)],
+                    sem.at[slot, t],
+                )
+                for t in range(chunk)
+            ]
 
         for slot in range(NBUF):
             @pl.when(slot < total)
             def _():
-                start(slot, slot)
+                for copy in copies(slot, slot):
+                    copy.start()
 
         def body(entry, carry):
             slot = entry % NBUF
             b = blk_ref[entry]
             c = chk_ref[entry]
-            pltpu.make_async_copy(
-                resp_hbm.at[:, :, 0, pl.ds(0, chunk)], buf.at[slot], sem.at[slot]
-            ).wait()
             count = live_ref[b]
             row = first + b
-            for t in range(chunk):
-                j = c * chunk + t
-
-                @pl.when(j < count)
-                def _():
-                    src = aper_ref[row * aper_w + j]
-                    for f in range(freq_dev):
-                        piece = g_ref[src, f]
-                        tile = buf[slot, f, :, t].reshape(2 * block_rows, block_cols)
-                        acc[b, f] += lax.dot_general(
-                            piece, tile, (((1,), (1,)), ((), ())),
-                            preferred_element_type=jnp.float32,
-                        )
+            for f in range(freq_dev):
+                for t in range(chunk):
+                    j = c * chunk + t
+                    src = jnp.maximum(aper_ref[row * aper_w + j], 0)
+                    piece = g_ref[src, f]
+                    pcat[f, pl.ds(t * block_cols, block_cols), :] = jnp.where(
+                        j < count, piece, jnp.zeros_like(piece)
+                    )
+            for copy in copies(entry, slot):
+                copy.wait()
+            for f in range(freq_dev):
+                tiles = buf[slot, f].reshape(2 * block_rows, chunk * block_cols)
+                acc[b, f] += jnp.dot(tiles, pcat[f], preferred_element_type=jnp.float32)
 
             @pl.when(entry + NBUF < total)
             def _():
-                start(entry + NBUF, slot)
+                for copy in copies(entry + NBUF, slot):
+                    copy.start()
 
             return carry
 
@@ -95,7 +99,7 @@
 
         for b in range(blk_dev):
             for f in range(freq_dev):
-                v = acc[b, f]
+                v = acc[b, f].T
                 p00 = v[0:focal, 0:block_rows]
                 p01 = v[0:focal, block_rows:]
                 p10 = v[focal:, 0:block_rows]
@@ -120,9 +124,10 @@
         in_specs=[smem, smem, smem, smem, smem, pl.BlockSpec(memory_space=pl.ANY), vmem],
         out_specs=vmem,
         scratch_shapes=[
-            pltpu.VMEM((NBUF, freq_dev, 2, chunk, block_rows, block_cols), response.dtype),
-            pltpu.SemaphoreType.DMA((NBUF,)),
-            pltpu.VMEM((blk_dev, freq_dev, rows_g, 2 * block_rows), jnp.float32),
+            pltpu.VMEM((NBUF, freq_dev, 2, block_rows, chunk * block_cols), response.dtype),
+            pltpu.SemaphoreType.DMA((NBUF, chunk)),
+            pltpu.VMEM((freq_dev, chunk * block_cols, rows_g), response.dtype),
+            pltpu.VMEM((blk_dev, freq_dev, 2 * block_rows, rows_g), jnp.float32),
         ],
     )(flat_aperture, blocks, chunks, meta, live, response, gathered)
 
@@ -131,7 +136,7 @@
     freq_dev, unused, focal, traces = spectra.shape
     blk_dev = traces // block_rows
     local = spectra.reshape(freq_dev, 2 * focal, blk_dev, block_rows)
-    local = jnp.transpose(local, (2, 0, 1, 3))
+    local = jnp.transpose(local, (2, 0, 3, 1))
     return lax.all_gather(local, "rblk", axis=0, tiled=True)
 
 

time: 153 us -> 140 us (0.915); the launches traced: 152 us -> 137 us
  Pallas kernels: 59.9 us -> 38.5 us
  local copies, waits for them, and re-layouts: 4.6 us -> 11.6 us
    pallas_call x2, Pallas kernels: 59.9 us -> 38.5 us  [block_products(): pl.pallas_call(kernel, out_shape=jax.ShapeDtypeStruct((freq_dev, 2, focal...]
    all_gather x0 -> x2, local copies, waits for them, and re-layouts: none -> 6.31 us  [gather_columns(): return lax.all_gather(local, 'rblk', axis=0, tiled=True)]
    all_gather x2, blocking collectives: 29.1 us -> 26.8 us  [gather_columns(): return lax.all_gather(local, 'rblk', axis=0, tiled=True)]
where the time goes in v1:
time: 140 us; the launch traced here: 137 us
  blocking collectives  66.2 us (47%)
  Pallas kernels  38.5 us (28%)
  other arithmetic  19.6 us (14%)
  local copies, waits for them, and re-layouts  11.6 us (8%)
  between operations  1.47 us (1%)
    unnamed x2, blocking collectives  39.3 us
    pallas_call x2, Pallas kernels, block_products(): pl.pallas_call(kernel, out_shape=jax.ShapeDtypeStruct((freq_dev, 2, focal...  38.5 us
    all_gather x2, blocking collectives, gather_columns(): return lax.all_gather(local, 'rblk', axis=0, tiled=True)  26.8 us
    reduce_sum x2, other arithmetic, apply_window(): new_real = jnp.sum(real_in * c_rr + imag_in * c_ir, axis=0)  8.35 us
    all_gather x2, local copies, waits for them, and re-layouts, gather_columns(): return lax.all_gather(local, 'rblk', axis=0, tiled=True)  6.31 us
    min x1, other arithmetic, chunk_schedule(): chunks = jnp.clip(entry - starts[blocks], 0, per_blk - 1)  5.54 us

profile of v1, /device:TPU:8, one launch (start us, length us, event | category | flops | bytes accessed | tf_op | source)
XLA Modules:
  0.0 137.4 jit_solution(17150087020319248721)
XLA Ops:
  0.7 0.8 convert_reduce_fusion.live_ref
  1.5 1.2 dynamic-slice
  3.4 0.1 fusion.27
  3.5 0.2 reduce-window.4
  3.7 0.6 slice.19
  4.3 1.3 pad_add_fusion.meta_ref
  5.6 0.1 convert_reduce_fusion.1
  5.6 0.1 sine_select_fusion
  5.8 0.1 add_negate_fusion
  5.8 0.7 fusion.33
  6.5 5.5 %fusion.31 = (s32[56]{0:T(128)}, s32[56]{0:T(128)}) fusion(s32[]{:T(128)} %bitcast.6, s32[]{:T(128)} %bitcast.7, s32[]{:T(128)} %bitcast.8, s32[]{:T(128)} %bitcast.9, s32[]{:T(128)} %bitcast.10, s32[]{:T(128)} %bitcast.12, s32[]{:T(128)} %bitcast.11, s32[]{:T(128)} %bitcast.5, s32[56]{0:T(128)S(1)} %convert_reduce_fusion.1), kind=kLoop, calls=%fused_computation.99 | loop fusion | flops 1120 | bytes 704 | tf_op jit(solution)/shard_map/jit(clip)/min | solution.py:34
  12.1 0.8 copy.14
  12.9 0.7 reshape.348.aper_ref
  13.6 0.8 reshape.349
  14.4 0.8 fusion.32
  15.2 14.4 %all_gather.6 = bf16[64,2,128,8]{2,3,1,0:T(8,128)(2,1)S(1)} all-gather(bf16[8,2,128,8]{2,3,1,0:T(8,128)(2,1)S(1)} %copy.15), channel_id=1, replica_groups=mesh['freq'=4,'rblk'=8] {'rblk'}, dimensions={0}, use_global_device_ids=true | all-gather | bytes 294912 | tf_op jit(solution)/shard_map/all_gather | solution.py:140
  29.6 3.2 %copy.16.g_ref = bf16[64,2,128,8]{3,2,1,0:T(8,128)(2,1)} copy(bf16[64,2,128,8]{2,3,1,0:T(8,128)(2,1)S(1)} %all_gather.6) | data formatting | bytes 524288 | tf_op jit(solution)/shard_map/all_gather | solution.py:140
  32.8 19.2 %shard_map.59 = bf16[2,2,4,1024]{3,2,1,0:T(4,128)(2,1)} custom-call(s32[3136]{0:T(1024)} %reshape.348.aper_ref, s32[56]{0:T(128)} %get-tuple-element.21.blk_ref, s32[56]{0:T(128)} %get-tuple-element.20.chk_ref, s32[2]{0:T(128)} %pad_add_fusion.meta_ref, s32[8]{0:T(128)} %copy-done.3, bf16[2,2,8,49,128,128]{5,4,3,2,1,0:T(8,128)(2,1)} %resp_hbm.3, ...), custom_call_target="tpu_custom_call" | custom-call | tf_op jit(solution)/shard_map/pallas_call | solution.py:119
  52.0 0.8 convert_element_type.72
  52.8 0.0 copy-done.2
  52.8 4.2 %add_reduce_fusion.3 = (f32[8,4,1024]{2,0,1:T(8,128)S(1)}, f32[8,4,1024]{2,0,1:T(8,128)S(1)}) fusion(f32[2,4,1024]{2,1,0:T(4,128)S(1)} %get-tuple-element.11, f32[2,4,1024]{2,1,0:T(4,128)S(1)} %get-tuple-element.10, f32[2,8]{1,0:T(2,128)S(1)} %get-tuple-element.19, s32[2,8]{1,0:T(2,128)S(1)} %get-tuple-element.17, pred[2,8]{1,0:T(4,128)(4,1)S(1)} %get-tuple-element.15, ...), kind=kLoop, calls=%fused_computation.43 | loop fusion | flops 4915200 | bytes 377120 | tf_op jit(solution)/shard_map/reduce_sum | solution.py:182
  57.0 0.2 copy.17
  57.2 20.3 %all-reduce.4 = bf16[8,2,4,1024]{3,2,1,0:T(4,128)(2,1)S(1)} all-reduce(f32[8,2,4,1024]{3,2,1,0:T(4,128)S(1)} %copy.17), channel_id=2, replica_groups=mesh['freq'=4,'rblk'=8] {'freq'}, use_global_device_ids=true, to_apply=%region_5.6.clone | all-reduce | flops 65536 | bytes 393216
  77.5 0.0 copy-start.1
  77.5 12.4 %all_gather.7 = bf16[64,2,128,8]{2,3,1,0:T(8,128)(2,1)S(1)} all-gather(bf16[8,2,128,8]{2,3,1,0:T(8,128)(2,1)S(1)} %copy.18), channel_id=1, replica_groups=mesh['freq'=4,'rblk'=8] {'rblk'}, dimensions={0}, use_global_device_ids=true | all-gather | bytes 294912 | tf_op jit(solution)/shard_map/all_gather | solution.py:140
  89.9 3.2 %copy.19.g_ref = bf16[64,2,128,8]{3,2,1,0:T(8,128)(2,1)} copy(bf16[64,2,128,8]{2,3,1,0:T(8,128)(2,1)S(1)} %all_gather.7) | data formatting | bytes 524288 | tf_op jit(solution)/shard_map/all_gather | solution.py:140
  93.1 19.4 %shard_map.60 = bf16[2,2,4,1024]{3,2,1,0:T(4,128)(2,1)} custom-call(s32[3136]{0:T(1024)} %reshape.348.aper_ref, s32[56]{0:T(128)} %get-tuple-element.21.blk_ref, s32[56]{0:T(128)} %get-tuple-element.20.chk_ref, s32[2]{0:T(128)} %pad_add_fusion.meta_ref, s32[8]{0:T(128)} %copy-done.3, bf16[2,2,8,49,128,128]{5,4,3,2,1,0:T(8,128)(2,1)} %resp_hbm.3, ...), custom_call_target="tpu_custom_call" | custom-call | tf_op jit(solution)/shard_map/pallas_call | solution.py:119
  112.5 0.8 convert_element_type.74
  113.2 4.2 %add_reduce_fusion.1 = (f32[8,4,1024]{2,0,1:T(8,128)S(1)}, f32[8,4,1024]{2,0,1:T(8,128)S(1)}) fusion(f32[2,4,1024]{2,1,0:T(4,128)S(1)} %get-tuple-element.9, f32[2,4,1024]{2,1,0:T(4,128)S(1)} %get-tuple-element.8, f32[2,8]{1,0:T(2,128)S(1)} %get-tuple-element.19, s32[2,8]{1,0:T(2,128)S(1)} %get-tuple-element.17, pred[2,8]{1,0:T(4,128)(4,1)S(1)} %get-tuple-element.15, ...), kind=kLoop, calls=%fused_computation.41 | loop fusion | flops 4915200 | bytes 377120 | tf_op jit(solution)/shard_map/reduce_sum | solution.py:182
  117.5 0.2 copy.20
  117.6 19.1 %all-reduce.5 = bf16[8,2,4,1024]{3,2,1,0:T(4,128)(2,1)S(1)} all-reduce(f32[8,2,4,1024]{3,2,1,0:T(4,128)S(1)} %copy.20), channel_id=3, replica_groups=mesh['freq'=4,'rblk'=8] {'freq'}, use_global_device_ids=true, to_apply=%region_8.9.clone | all-reduce | flops 65536 | bytes 393216
  136.7 0.6 add_convert_fusion
  (18 shorter events, 0.2 us)
Async XLA Ops:
  1.5 31.3 %copy-start.3 = (s32[8]{0:T(128)}, s32[8]{0:T(128)S(1)}, u32[]{:S(2)}) copy-start(s32[8]{0:T(128)S(1)} %convert_reduce_fusion.live_ref) | copy-start | bytes 100
  32.8 20.0 %copy-start.2 = (s32[4,1024]{1,0:T(4,128)S(1)}, s32[4,1024]{1,0:T(4,128)}, u32[]{:S(2)}) copy-start(s32[4,1024]{1,0:T(4,128)} %param.7) | copy-start | bytes 49156
  77.5 35.0 %copy-start.1 = (bf16[2,2,4,1024]{3,2,1,0:T(4,128)(2,1)}, bf16[2,2,4,1024]{3,2,1,0:T(4,128)(2,1)S(1)}, u32[]{:S(2)}) copy-start(bf16[2,2,4,1024]{3,2,1,0:T(4,128)(2,1)S(1)} %dynamic-slice_convert_fusion.1) | copy-start | bytes 98308
  93.1 43.6 %copy-start = (bf16[2,2,4,1024]{3,2,1,0:T(4,128)(2,1)S(1)}, bf16[2,2,4,1024]{3,2,1,0:T(4,128)(2,1)}, u32[]{:S(2)}) copy-start(bf16[2,2,4,1024]{3,2,1,0:T(4,128)(2,1)} %param.6) | copy-start | bytes 98308

commit v2 on v1

--- a/solution.py
+++ b/solution.py
@@ -182,7 +182,15 @@
     new_real = jnp.sum(real_in * c_rr + imag_in * c_ir, axis=0)
     new_imag = jnp.sum(real_in * c_ri + imag_in * c_ii, axis=0)
     partial = jnp.stack([new_real, new_imag], axis=1)
-    summed = lax.psum_scatter(partial, "freq", scatter_dimension=0, tiled=True)
+    freq_dev = spectra.shape[0]
+    count = lax.axis_size("freq")
+    me = lax.axis_index("freq")
+    summed = lax.dynamic_slice_in_dim(partial, me * freq_dev, freq_dev, 0)
+    for shift in range(1, count):
+        target = (me + shift) % count
+        outgoing = lax.dynamic_slice_in_dim(partial, target * freq_dev, freq_dev, 0)
+        pairs = [(i, (i + shift) % count) for i in range(count)]
+        summed = summed + lax.ppermute(outgoing, "freq", pairs)
     return summed.astype(jnp.bfloat16)
 
 

time: 140 us -> 112 us (0.80)
  blocking collectives: 66.2 us -> 27 us
  starting transfers between devices: 0 us -> 7.97 us
  waiting for transfers between devices: 0 us -> 6.56 us
    unnamed x2 -> x0, blocking collectives: 39.3 us -> none
    ppermute x0 -> x6, starting transfers between devices: none -> 7.97 us  [apply_window(): summed = summed + lax.ppermute(outgoing, 'freq', pairs)]
    ppermute x0 -> x6, waiting for transfers between devices: none -> 6.56 us  [apply_window(): summed = summed + lax.ppermute(outgoing, 'freq', pairs)]
  transfers between devices with their start and end apart: 0 -> 6, of which waited for: 0 -> 6; matrix products, arithmetic and copies ran while one was open for 0% -> 0% of each run, Pallas kernels for 0% -> 0%
where the time goes in v2:
time: 112 us; the launch traced here: 110 us
  Pallas kernels  37.4 us (33%)
  blocking collectives  27 us (24%)
  other arithmetic  19.3 us (17%)
  local copies, waits for them, and re-layouts  10.7 us (10%)
  starting transfers between devices  7.97 us (7%)
  waiting for transfers between devices  6.56 us (6%)
    pallas_call x2, Pallas kernels, block_products(): pl.pallas_call(kernel, out_shape=jax.ShapeDtypeStruct((freq_dev, 2, focal...  37.4 us
    all_gather x2, blocking collectives, gather_columns(): return lax.all_gather(local, 'rblk', axis=0, tiled=True)  27 us
    reduce_sum x2, other arithmetic, apply_window(): new_imag = jnp.sum(real_in * c_ri + imag_in * c_ii, axis=0)  8.36 us
    ppermute x6, starting transfers between devices, apply_window(): summed = summed + lax.ppermute(outgoing, 'freq', pairs)  7.97 us
    ppermute x6, waiting for transfers between devices, apply_window(): summed = summed + lax.ppermute(outgoing, 'freq', pairs)  6.56 us
    all_gather x2, local copies, waits for them, and re-layouts, gather_columns(): return lax.all_gather(local, 'rblk', axis=0, tiled=True)  6.37 us
    min x1, other arithmetic, chunk_schedule(): chunks = jnp.clip(entry - starts[blocks], 0, per_blk - 1)  5.59 us
  transfers between devices with their start and end apart: 6, of which 6 were waited for; matrix products, arithmetic and copies ran while one was open for 0% of the time, Pallas kernels for 0%

profile of v2, /device:TPU:8, one launch (start us, length us, event | category | flops | bytes accessed | tf_op | source)
XLA Modules:
  0.0 109.8 jit_solution(9740189780694128051)
XLA Ops:
  1.0 0.8 copy.15
  1.8 0.8 convert_reduce_fusion.live_ref
  2.9 0.6 slice.19
  3.6 0.7 fusion.49
  4.3 0.7 reshape.348.aper_ref
  5.0 0.8 reshape.349
  5.8 0.8 fusion.48
  6.6 14.4 %all_gather.6 = bf16[64,2,128,8]{2,3,1,0:T(8,128)(2,1)S(1)} all-gather(bf16[8,2,128,8]{2,3,1,0:T(8,128)(2,1)S(1)} %copy.16), channel_id=1, replica_groups=mesh['freq'=4,'rblk'=8] {'rblk'}, dimensions={0}, use_global_device_ids=true | all-gather | bytes 294912 | tf_op jit(solution)/shard_map/all_gather | solution.py:140
  21.0 3.2 %copy.17.g_ref = bf16[64,2,128,8]{3,2,1,0:T(8,128)(2,1)} copy(bf16[64,2,128,8]{2,3,1,0:T(8,128)(2,1)S(1)} %all_gather.6) | data formatting | bytes 524288 | tf_op jit(solution)/shard_map/all_gather | solution.py:140
  24.2 1.3 %pad_add_fusion.meta_ref = s32[2]{0:T(128)} fusion(s32[1]{0:T(128)} %bitcast.15, s32[1]{0:T(128)} %bitcast.14), kind=kLoop, calls=%fused_computation.126 | loop fusion | flops 2 | bytes 16 | tf_op jit(solution)/shard_map/stack | solution.py:35
  25.4 5.6 %fusion.47 = (s32[56]{0:T(128)}, s32[56]{0:T(128)}) fusion(s32[]{:T(128)} %bitcast.6, s32[]{:T(128)} %bitcast.7, s32[]{:T(128)} %bitcast.8, s32[]{:T(128)} %bitcast.9, s32[]{:T(128)} %bitcast.10, s32[]{:T(128)} %bitcast.12, s32[]{:T(128)} %bitcast.11, s32[]{:T(128)} %bitcast.5, s32[56]{0:T(128)S(1)} %convert_reduce_fusion.1), kind=kLoop, calls=%fused_computation.127 | loop fusion | flops 1120 | bytes 704 | tf_op jit(solution)/shard_map/jit(clip)/min | solution.py:34
  31.0 18.6 %shard_map.59 = bf16[2,2,4,1024]{3,2,1,0:T(4,128)(2,1)} custom-call(s32[3136]{0:T(1024)} %reshape.348.aper_ref, s32[56]{0:T(128)} %get-tuple-element.29.blk_ref, s32[56]{0:T(128)} %get-tuple-element.28.chk_ref, s32[2]{0:T(128)} %pad_add_fusion.meta_ref, s32[8]{0:T(128)} %copy-done.3, bf16[2,2,8,49,128,128]{5,4,3,2,1,0:T(8,128)(2,1)} %resp_hbm.3, ...), custom_call_target="tpu_custom_call" | custom-call | tf_op jit(solution)/shard_map/pallas_call | solution.py:119
  49.7 0.8 convert_element_type.72
  50.5 4.2 %add_reduce_fusion.2 = (f32[8,4,1024]{2,0,1:T(8,128)S(1)}, f32[8,4,1024]{2,0,1:T(8,128)S(1)}) fusion(f32[2,4,1024]{2,1,0:T(4,128)S(1)} %get-tuple-element.19, f32[2,4,1024]{2,1,0:T(4,128)S(1)} %get-tuple-element.18, f32[2,8]{1,0:T(2,128)S(1)} %get-tuple-element.27, s32[2,8]{1,0:T(2,128)S(1)} %get-tuple-element.25, pred[2,8]{1,0:T(4,128)(4,1)S(1)} %get-tuple-element.23, ...), kind=kLoop, calls=%fused_computation.56 | loop fusion | flops 4915200 | bytes 377120 | tf_op jit(solution)/shard_map/reduce_sum | solution.py:183
  54.8 1.5 %collective-permute-start = (f32[2,2,4,1024]{3,0,2,1:T(2,128)S(1)}, f32[2,2,4,1024]{3,0,2,1:T(2,128)S(1)}, u32[]{:S(2)}, u32[]{:S(2)}) collective-permute-start(f32[2,2,4,1024]{3,0,2,1:T(2,128)S(1)} %get-tuple-element.13), channel_id=1, source_target_pairs={{0,8},{8,16},{16,24},{24,0},{1,9},{9,17},{17,25},{25,1},{2,10},{10... | collective-permute-start | bytes 196616 | tf_op jit(solution)/shard_map/ppermute | solution.py:193
  56.3 1.5 %collective-permute-start.1 = (f32[2,2,4,1024]{3,0,2,1:T(2,128)S(1)}, f32[2,2,4,1024]{3,0,2,1:T(2,128)S(1)}, u32[]{:S(2)}, u32[]{:S(2)}) collective-permute-start(f32[2,2,4,1024]{3,0,2,1:T(2,128)S(1)} %get-tuple-element.14), channel_id=1, source_target_pairs={{0,16},{8,24},{16,0},{24,8},{1,17},{9,25},{17,1},{25,9},{2,18},{10... | collective-permute-start | bytes 196616 | tf_op jit(solution)/shard_map/ppermute | solution.py:193
  57.8 1.4 %collective-permute-start.2 = (f32[2,2,4,1024]{3,0,2,1:T(2,128)S(1)}, f32[2,2,4,1024]{3,0,2,1:T(2,128)S(1)}, u32[]{:S(2)}, u32[]{:S(2)}) collective-permute-start(f32[2,2,4,1024]{3,0,2,1:T(2,128)S(1)} %get-tuple-element.15), channel_id=1, source_target_pairs={{0,24},{8,0},{16,8},{24,16},{1,25},{9,1},{17,9},{25,17},{2,26},{10... | collective-permute-start | bytes 196616 | tf_op jit(solution)/shard_map/ppermute | solution.py:193
  59.3 0.7 collective-permute-done
  60.0 0.7 collective-permute-done.1
  60.7 1.4 %collective-permute-done.2 = f32[2,2,4,1024]{3,0,2,1:T(2,128)S(1)} collective-permute-done((f32[2,2,4,1024]{3,0,2,1:T(2,128)S(1)}, f32[2,2,4,1024]{3,0,2,1:T(2,128)S(1)}, u32[]{:S(2)}, u32[]{:S(2)}) %collective-permute-start.2) | collective-permute-done | bytes 65568 | tf_op jit(solution)/shard_map/ppermute | solution.py:193
  62.2 12.6 %all_gather.7 = bf16[64,2,128,8]{2,3,1,0:T(8,128)(2,1)S(1)} all-gather(bf16[8,2,128,8]{2,3,1,0:T(8,128)(2,1)S(1)} %copy.19), channel_id=1, replica_groups=mesh['freq'=4,'rblk'=8] {'rblk'}, dimensions={0}, use_global_device_ids=true | all-gather | bytes 294912 | tf_op jit(solution)/shard_map/all_gather | solution.py:140
  74.8 3.2 %copy.20.g_ref = bf16[64,2,128,8]{3,2,1,0:T(8,128)(2,1)} copy(bf16[64,2,128,8]{2,3,1,0:T(8,128)(2,1)S(1)} %all_gather.7) | data formatting | bytes 524288 | tf_op jit(solution)/shard_map/all_gather | solution.py:140
  78.0 18.8 %shard_map.60 = bf16[2,2,4,1024]{3,2,1,0:T(4,128)(2,1)} custom-call(s32[3136]{0:T(1024)} %reshape.348.aper_ref, s32[56]{0:T(128)} %get-tuple-element.29.blk_ref, s32[56]{0:T(128)} %get-tuple-element.28.chk_ref, s32[2]{0:T(128)} %pad_add_fusion.meta_ref, s32[8]{0:T(128)} %copy-done.3, bf16[2,2,8,49,128,128]{5,4,3,2,1,0:T(8,128)(2,1)} %resp_hbm.3, ...), custom_call_target="tpu_custom_call" | custom-call | tf_op jit(solution)/shard_map/pallas_call | solution.py:119
  96.9 0.8 convert_element_type.74
  97.6 4.2 %add_reduce_fusion = (f32[8,4,1024]{2,0,1:T(8,128)S(1)}, f32[8,4,1024]{2,0,1:T(8,128)S(1)}) fusion(f32[2,4,1024]{2,1,0:T(4,128)S(1)} %get-tuple-element.17, f32[2,4,1024]{2,1,0:T(4,128)S(1)} %get-tuple-element.16, f32[2,8]{1,0:T(2,128)S(1)} %get-tuple-element.27, s32[2,8]{1,0:T(2,128)S(1)} %get-tuple-element.25, pred[2,8]{1,0:T(4,128)(4,1)S(1)} %get-tuple-element.23, ...), kind=kLoop, calls=%fused_computation.54 | loop fusion | flops 4915200 | bytes 377120 | tf_op jit(solution)/shard_map/reduce_sum | solution.py:183
  101.9 1.4 %collective-permute-start.3 = (f32[2,2,4,1024]{3,0,2,1:T(2,128)S(1)}, f32[2,2,4,1024]{3,0,2,1:T(2,128)S(1)}, u32[]{:S(2)}, u32[]{:S(2)}) collective-permute-start(f32[2,2,4,1024]{3,0,2,1:T(2,128)S(1)} %get-tuple-element.10), channel_id=1, source_target_pairs={{0,8},{8,16},{16,24},{24,0},{1,9},{9,17},{17,25},{25,1},{2,10},{10... | collective-permute-start | bytes 196616 | tf_op jit(solution)/shard_map/ppermute | solution.py:193
  103.3 1.5 %collective-permute-start.4 = (f32[2,2,4,1024]{3,0,2,1:T(2,128)S(1)}, f32[2,2,4,1024]{3,0,2,1:T(2,128)S(1)}, u32[]{:S(2)}, u32[]{:S(2)}) collective-permute-start(f32[2,2,4,1024]{3,0,2,1:T(2,128)S(1)} %get-tuple-element.11), channel_id=1, source_target_pairs={{0,16},{8,24},{16,0},{24,8},{1,17},{9,25},{17,1},{25,9},{2,18},{10... | collective-permute-start | bytes 196616 | tf_op jit(solution)/shard_map/ppermute | solution.py:193
  104.9 0.5 collective-permute-start.5
  105.4 1.8 %collective-permute-done.3 = f32[2,2,4,1024]{3,0,2,1:T(2,128)S(1)} collective-permute-done((f32[2,2,4,1024]{3,0,2,1:T(2,128)S(1)}, f32[2,2,4,1024]{3,0,2,1:T(2,128)S(1)}, u32[]{:S(2)}, u32[]{:S(2)}) %collective-permute-start.3) | collective-permute-done | bytes 65568 | tf_op jit(solution)/shard_map/ppermute | solution.py:193
  107.1 0.7 collective-permute-done.4
  107.8 1.3 %collective-permute-done.5 = f32[2,2,4,1024]{3,0,2,1:T(2,128)S(1)} collective-permute-done((f32[2,2,4,1024]{3,0,2,1:T(2,128)S(1)}, f32[2,2,4,1024]{3,0,2,1:T(2,128)S(1)}, u32[]{:S(2)}, u32[]{:S(2)}) %collective-permute-start.5) | collective-permute-done | bytes 65568 | tf_op jit(solution)/shard_map/ppermute | solution.py:193
  109.2 0.6 copy.21
  (27 shorter events, 1.0 us)
Async XLA Ops:
  2.7 28.4 %copy-start.3 = (s32[8]{0:T(128)}, s32[8]{0:T(128)S(1)}, u32[]{:S(2)}) copy-start(s32[8]{0:T(128)S(1)} %convert_reduce_fusion.live_ref) | copy-start | bytes 100
  31.0 19.4 %copy-start.2 = (s32[4,1024]{1,0:T(4,128)S(1)}, s32[4,1024]{1,0:T(4,128)}, u32[]{:S(2)}) copy-start(s32[4,1024]{1,0:T(4,128)} %param.7) | copy-start | bytes 49156
  54.8 5.2 %collective-permute-start = (f32[2,2,4,1024]{3,0,2,1:T(2,128)S(1)}, f32[2,2,4,1024]{3,0,2,1:T(2,128)S(1)}, u32[]{:S(2)}, u32[]{:S(2)}) collective-permute-start(f32[2,2,4,1024]{3,0,2,1:T(2,128)S(1)} %get-tuple-element.13), channel_id=1, source_target_pairs={{0,8},{8,16},{16,24},{24,0},{1,9},{9,17},{17,25},{25,1},{2,10},{10... | collective-permute-start | bytes 196616 | tf_op jit(solution)/shard_map/ppermute | solution.py:193
  56.3 4.4 %collective-permute-start.1 = (f32[2,2,4,1024]{3,0,2,1:T(2,128)S(1)}, f32[2,2,4,1024]{3,0,2,1:T(2,128)S(1)}, u32[]{:S(2)}, u32[]{:S(2)}) collective-permute-start(f32[2,2,4,1024]{3,0,2,1:T(2,128)S(1)} %get-tuple-element.14), channel_id=1, source_target_pairs={{0,16},{8,24},{16,0},{24,8},{1,17},{9,25},{17,1},{25,9},{2,18},{10... | collective-permute-start | bytes 196616 | tf_op jit(solution)/shard_map/ppermute | solution.py:193
  57.8 4.3 %collective-permute-start.2 = (f32[2,2,4,1024]{3,0,2,1:T(2,128)S(1)}, f32[2,2,4,1024]{3,0,2,1:T(2,128)S(1)}, u32[]{:S(2)}, u32[]{:S(2)}) collective-permute-start(f32[2,2,4,1024]{3,0,2,1:T(2,128)S(1)} %get-tuple-element.15), channel_id=1, source_target_pairs={{0,24},{8,0},{16,8},{24,16},{1,25},{9,1},{17,9},{25,17},{2,26},{10... | collective-permute-start | bytes 196616 | tf_op jit(solution)/shard_map/ppermute | solution.py:193
  62.2 34.7 %copy-start.1 = (bf16[2,2,4,1024]{3,2,1,0:T(4,128)(2,1)}, bf16[2,2,4,1024]{3,2,1,0:T(4,128)(2,1)S(1)}, u32[]{:S(2)}) copy-start(bf16[2,2,4,1024]{3,2,1,0:T(4,128)(2,1)S(1)} %copy.18) | copy-start | bytes 98308
  78.0 31.1 %copy-start = (bf16[2,2,4,1024]{3,2,1,0:T(4,128)(2,1)S(1)}, bf16[2,2,4,1024]{3,2,1,0:T(4,128)(2,1)}, u32[]{:S(2)}) copy-start(bf16[2,2,4,1024]{3,2,1,0:T(4,128)(2,1)} %param.6) | copy-start | bytes 98308
  101.9 5.2 %collective-permute-start.3 = (f32[2,2,4,1024]{3,0,2,1:T(2,128)S(1)}, f32[2,2,4,1024]{3,0,2,1:T(2,128)S(1)}, u32[]{:S(2)}, u32[]{:S(2)}) collective-permute-start(f32[2,2,4,1024]{3,0,2,1:T(2,128)S(1)} %get-tuple-element.10), channel_id=1, source_target_pairs={{0,8},{8,16},{16,24},{24,0},{1,9},{9,17},{17,25},{25,1},{2,10},{10... | collective-permute-start | bytes 196616 | tf_op jit(solution)/shard_map/ppermute | solution.py:193
  103.3 4.5 %collective-permute-start.4 = (f32[2,2,4,1024]{3,0,2,1:T(2,128)S(1)}, f32[2,2,4,1024]{3,0,2,1:T(2,128)S(1)}, u32[]{:S(2)}, u32[]{:S(2)}) collective-permute-start(f32[2,2,4,1024]{3,0,2,1:T(2,128)S(1)} %get-tuple-element.11), channel_id=1, source_target_pairs={{0,16},{8,24},{16,0},{24,8},{1,17},{9,25},{17,1},{25,9},{2,18},{10... | collective-permute-start | bytes 196616 | tf_op jit(solution)/shard_map/ppermute | solution.py:193
  104.9 4.3 %collective-permute-start.5 = (f32[2,2,4,1024]{3,0,2,1:T(2,128)S(1)}, f32[2,2,4,1024]{3,0,2,1:T(2,128)S(1)}, u32[]{:S(2)}, u32[]{:S(2)}) collective-permute-start(f32[2,2,4,1024]{3,0,2,1:T(2,128)S(1)} %get-tuple-element.12), channel_id=1, source_target_pairs={{0,24},{8,0},{16,8},{24,16},{1,25},{9,1},{17,9},{25,17},{2,26},{10... | collective-permute-start | bytes 196616 | tf_op jit(solution)/shard_map/ppermute | solution.py:193

commit v3 on v2

--- a/solution.py
+++ b/solution.py
@@ -38,7 +38,7 @@
 
 def block_products(gathered, response, aperture, first_block, conjugate):
     freq_dev, unused, blk_dev, aper_w, block_rows, block_cols = response.shape
-    rows_g = gathered.shape[3]
+    rows_g = gathered.shape[2]
     chunk = chunk_width(aper_w)
     blocks, chunks, meta, live = chunk_schedule(aperture, first_block, blk_dev, chunk)
     flat_aperture = aperture.reshape(-1)
@@ -79,14 +79,17 @@
                     j = c * chunk + t
                     src = jnp.maximum(aper_ref[row * aper_w + j], 0)
                     piece = g_ref[src, f]
-                    pcat[f, pl.ds(t * block_cols, block_cols), :] = jnp.where(
+                    pcat[f, :, pl.ds(t * block_cols, block_cols)] = jnp.where(
                         j < count, piece, jnp.zeros_like(piece)
                     )
             for copy in copies(entry, slot):
                 copy.wait()
             for f in range(freq_dev):
                 tiles = buf[slot, f].reshape(2 * block_rows, chunk * block_cols)
-                acc[b, f] += jnp.dot(tiles, pcat[f], preferred_element_type=jnp.float32)
+                acc[b, f] += lax.dot_general(
+                    tiles, pcat[f], (((1,), (1,)), ((), ())),
+                    preferred_element_type=jnp.float32,
+                )
 
             @pl.when(entry + NBUF < total)
             def _():
@@ -126,7 +129,7 @@
         scratch_shapes=[
             pltpu.VMEM((NBUF, freq_dev, 2, block_rows, chunk * block_cols), response.dtype),
             pltpu.SemaphoreType.DMA((NBUF, chunk)),
-            pltpu.VMEM((freq_dev, chunk * block_cols, rows_g), response.dtype),
+            pltpu.VMEM((freq_dev, rows_g, chunk * block_cols), response.dtype),
             pltpu.VMEM((blk_dev, freq_dev, 2 * block_rows, rows_g), jnp.float32),
         ],
     )(flat_aperture, blocks, chunks, meta, live, response, gathered)
@@ -136,8 +139,25 @@
     freq_dev, unused, focal, traces = spectra.shape
     blk_dev = traces // block_rows
     local = spectra.reshape(freq_dev, 2 * focal, blk_dev, block_rows)
-    local = jnp.transpose(local, (2, 0, 3, 1))
-    return lax.all_gather(local, "rblk", axis=0, tiled=True)
+    local = jnp.transpose(local, (2, 0, 1, 3))
+    count = lax.axis_size("rblk")
+    if count & (count - 1):
+        return lax.all_gather(local, "rblk", axis=0, tiled=True)
+    step = 1
+    while step < count:
+        pairs = [(i, i ^ step) for i in range(count)]
+        local = jnp.concatenate([local, lax.ppermute(local, "rblk", pairs)], axis=0)
+        step *= 2
+    return local
+
+
+def arrival_order(aperture, blk_dev):
+    count = lax.axis_size("rblk")
+    if count & (count - 1):
+        return aperture
+    me = lax.axis_index("rblk")
+    place = jnp.bitwise_xor(me, aperture // blk_dev)
+    return jnp.where(aperture >= 0, place * blk_dev + aperture % blk_dev, aperture)
 
 
 def dirichlet(offsets, limits):
@@ -201,14 +221,15 @@
     freq_all = freq_dev * lax.axis_size("freq")
     first_block = lax.axis_index("rblk") * blk_dev
     tables = window_tables(arrival, freq_dev, freq_all)
+    ordered = arrival_order(aperture, blk_dev)
     current = focus_init
     window_q = focus_init
     for iteration in range(ITERS):
         gathered = gather_columns(current, block_rows)
-        forward = block_products(gathered, response, aperture, first_block, False)
+        forward = block_products(gathered, response, ordered, first_block, False)
         window_q = apply_window(forward, tables)
         mirrored = gather_columns(window_q, block_rows)
-        adjoint = block_products(mirrored, response, aperture, first_block, True)
+        adjoint = block_products(mirrored, response, ordered, first_block, True)
         windowed = apply_window(adjoint, tables)
         current = (focus_init.astype(jnp.float32) + windowed.astype(jnp.float32)).astype(
             jnp.bfloat16

time: 112 us -> 96.6 us (0.86)
  blocking collectives: 27 us -> 0 us
  waiting for transfers between devices: 6.56 us -> 21.8 us
  local copies, waits for them, and re-layouts: 10.7 us -> 3.55 us
  starting transfers between devices: 7.97 us -> 11 us
  other arithmetic: 19.3 us -> 20.9 us
    all_gather x2 -> x0, blocking collectives: 27 us -> none  [gather_columns(): return lax.all_gather(local, 'rblk', axis=0, tiled=True)]
    ppermute x0 -> x6, waiting for transfers between devices: none -> 15.2 us  [gather_columns(): local = jnp.concatenate([local, lax.ppermute(local, 'rblk', pairs)], axis=0)]
    all_gather x2 -> x0, local copies, waits for them, and re-layouts: 6.37 us -> none  [gather_columns(): return lax.all_gather(local, 'rblk', axis=0, tiled=True)]
    ppermute x0 -> x6, starting transfers between devices: none -> 3.01 us  [gather_columns(): local = jnp.concatenate([local, lax.ppermute(local, 'rblk', pairs)], axis=0)]
    concatenate x0 -> x6, other arithmetic: none -> 1.49 us  [gather_columns(): local = jnp.concatenate([local, lax.ppermute(local, 'rblk', pairs)], axis=0)]
  transfers between devices with their start and end apart: 6 -> 12, of which waited for: 6 -> 10; matrix products, arithmetic and copies ran while one was open for 0% -> 12% of each run, Pallas kernels for 0% -> 0%
where the time goes in v3:
time: 96.6 us; the launch traced here: 95.4 us
  Pallas kernels  37.4 us (39%)
  waiting for transfers between devices  21.8 us (23%)
  other arithmetic  20.9 us (22%)
  starting transfers between devices  11 us (11%)
  local copies, waits for them, and re-layouts  3.55 us (4%)
    pallas_call x2, Pallas kernels, block_products(): pl.pallas_call(kernel, out_shape=jax.ShapeDtypeStruct((freq_dev, 2, focal...  37.4 us
    ppermute x6, waiting for transfers between devices, gather_columns(): local = jnp.concatenate([local, lax.ppermute(local, 'rblk', pairs)], axis=0)  15.2 us
    reduce_sum x2, other arithmetic, apply_window(): new_imag = jnp.sum(real_in * c_ri + imag_in * c_ii, axis=0)  8.36 us
    ppermute x6, starting transfers between devices, apply_window(): summed = summed + lax.ppermute(outgoing, 'freq', pairs)  7.97 us
    ppermute x6, waiting for transfers between devices, apply_window(): summed = summed + lax.ppermute(outgoing, 'freq', pairs)  6.57 us
    min x1, other arithmetic, chunk_schedule(): chunks = jnp.clip(entry - starts[blocks], 0, per_blk - 1)  5.6 us
    ppermute x6, starting transfers between devices, gather_columns(): local = jnp.concatenate([local, lax.ppermute(local, 'rblk', pairs)], axis=0)  3.01 us
  transfers between devices with their start and end apart: 12, of which 10 were waited for; matrix products, arithmetic and copies ran while one was open for 12% of the time, Pallas kernels for 0%

profile of v3, /device:TPU:8, one launch (start us, length us, event | category | flops | bytes accessed | tf_op | source)
XLA Modules:
  0.0 95.4 jit_solution(1321426798490447136)
XLA Ops:
  0.6 0.8 reshape.349
  1.8 0.8 compare_select_fusion
  2.9 0.8 fusion.54
  3.9 0.7 fusion.55
  4.6 3.8 %collective-permute-done.1 = bf16[16,2,8,128]{3,2,1,0:T(8,128)(2,1)S(1)} collective-permute-done((bf16[16,2,8,128]{3,2,1,0:T(8,128)(2,1)S(1)}, bf16[16,2,8,128]{3,2,1,0:T(8,128)(2,1)S(1)}, u32[]{:S(2)}, u32[]{:S(2)}) %collective-permute-start.1) | collective-permute-done | bytes 65568 | tf_op jit(solution)/shard_map/ppermute | solution.py:149
  8.4 2.7 %collective-permute-start.2 = (bf16[32,2,8,128]{3,2,1,0:T(8,128)(2,1)S(1)}, bf16[32,2,8,128]{3,2,1,0:T(8,128)(2,1)S(1)}, u32[]{:S(2)}, u32[]{:S(2)}) collective-permute-start(bf16[32,2,8,128]{3,2,1,0:T(8,128)(2,1)S(1)} %pad_maximum_fusion.2), channel_id=1, source_target_pairs={{0,4},{1,5},{2,6},{3,7},{4,0},{5,1},{6,2},{7,3},{8,12},{9,13},{10,... | collective-permute-start | bytes 393224 | tf_op jit(solution)/shard_map/ppermute | solution.py:149
  11.1 5.6 %fusion.53 = (s32[56]{0:T(128)}, s32[56]{0:T(128)}) fusion(s32[]{:T(128)} %bitcast.6, s32[]{:T(128)} %bitcast.7, s32[]{:T(128)} %bitcast.8, s32[]{:T(128)} %bitcast.9, s32[]{:T(128)} %bitcast.10, s32[]{:T(128)} %bitcast.12, s32[]{:T(128)} %bitcast.11, s32[]{:T(128)} %bitcast.5, s32[56]{0:T(128)S(1)} %convert_reduce_fusion.1), kind=kLoop, calls=%fused_computation.148 | loop fusion | flops 1120 | bytes 704 | tf_op jit(solution)/shard_map/jit(clip)/min | solution.py:34
  17.3 0.7 reshape.348.aper_ref
  18.1 1.3 %pad_add_fusion.meta_ref = s32[2]{0:T(128)} fusion(s32[1]{0:T(128)} %bitcast.15, s32[1]{0:T(128)} %bitcast.14), kind=kLoop, calls=%fused_computation.147 | loop fusion | flops 2 | bytes 16 | tf_op jit(solution)/shard_map/stack | solution.py:35
  19.4 0.7 pad_maximum_fusion.g_ref
  20.1 18.6 %shard_map.59 = bf16[2,2,4,1024]{3,2,1,0:T(4,128)(2,1)} custom-call(s32[3136]{0:T(1024)} %reshape.348.aper_ref, s32[56]{0:T(128)} %get-tuple-element.29.blk_ref, s32[56]{0:T(128)} %get-tuple-element.28.chk_ref, s32[2]{0:T(128)} %pad_add_fusion.meta_ref, s32[8]{0:T(128)} %copy-done.3, bf16[2,2,8,49,128,128]{5,4,3,2,1,0:T(8,128)(2,1)} %resp_hbm.3, ...), custom_call_target="tpu_custom_call" | custom-call | tf_op jit(solution)/shard_map/pallas_call | solution.py:122
  38.8 0.8 convert_element_type.72
  39.5 4.2 %add_reduce_fusion.2 = (f32[8,4,1024]{2,0,1:T(8,128)S(1)}, f32[8,4,1024]{2,0,1:T(8,128)S(1)}) fusion(f32[2,4,1024]{2,1,0:T(4,128)S(1)} %get-tuple-element.19, f32[2,4,1024]{2,1,0:T(4,128)S(1)} %get-tuple-element.18, f32[2,8]{1,0:T(2,128)S(1)} %get-tuple-element.27, s32[2,8]{1,0:T(2,128)S(1)} %get-tuple-element.25, pred[2,8]{1,0:T(4,128)(4,1)S(1)} %get-tuple-element.23, ...), kind=kLoop, calls=%fused_computation.58 | loop fusion | flops 4915200 | bytes 377120 | tf_op jit(solution)/shard_map/reduce_sum | solution.py:203
  43.8 1.5 %collective-permute-start.3 = (f32[2,2,4,1024]{3,0,2,1:T(2,128)S(1)}, f32[2,2,4,1024]{3,0,2,1:T(2,128)S(1)}, u32[]{:S(2)}, u32[]{:S(2)}) collective-permute-start(f32[2,2,4,1024]{3,0,2,1:T(2,128)S(1)} %get-tuple-element.13), channel_id=1, source_target_pairs={{0,8},{8,16},{16,24},{24,0},{1,9},{9,17},{17,25},{25,1},{2,10},{10... | collective-permute-start | bytes 196616 | tf_op jit(solution)/shard_map/ppermute | solution.py:213
  45.4 1.5 %collective-permute-start.4 = (f32[2,2,4,1024]{3,0,2,1:T(2,128)S(1)}, f32[2,2,4,1024]{3,0,2,1:T(2,128)S(1)}, u32[]{:S(2)}, u32[]{:S(2)}) collective-permute-start(f32[2,2,4,1024]{3,0,2,1:T(2,128)S(1)} %get-tuple-element.14), channel_id=1, source_target_pairs={{0,16},{8,24},{16,0},{24,8},{1,17},{9,25},{17,1},{25,9},{2,18},{10... | collective-permute-start | bytes 196616 | tf_op jit(solution)/shard_map/ppermute | solution.py:213
  46.9 1.4 %collective-permute-start.5 = (f32[2,2,4,1024]{3,0,2,1:T(2,128)S(1)}, f32[2,2,4,1024]{3,0,2,1:T(2,128)S(1)}, u32[]{:S(2)}, u32[]{:S(2)}) collective-permute-start(f32[2,2,4,1024]{3,0,2,1:T(2,128)S(1)} %get-tuple-element.15), channel_id=1, source_target_pairs={{0,24},{8,0},{16,8},{24,16},{1,25},{9,1},{17,9},{25,17},{2,26},{10... | collective-permute-start | bytes 196616 | tf_op jit(solution)/shard_map/ppermute | solution.py:213
  48.3 0.7 collective-permute-done.3
  49.0 0.7 collective-permute-done.4
  49.7 1.4 %collective-permute-done.5 = f32[2,2,4,1024]{3,0,2,1:T(2,128)S(1)} collective-permute-done((f32[2,2,4,1024]{3,0,2,1:T(2,128)S(1)}, f32[2,2,4,1024]{3,0,2,1:T(2,128)S(1)}, u32[]{:S(2)}, u32[]{:S(2)}) %collective-permute-start.5) | collective-permute-done | bytes 65568 | tf_op jit(solution)/shard_map/ppermute | solution.py:213
  51.4 1.2 %collective-permute-done.6 = bf16[8,2,8,128]{3,2,1,0:T(8,128)(2,1)S(1)} collective-permute-done((bf16[8,2,8,128]{3,2,1,0:T(8,128)(2,1)S(1)}, bf16[8,2,8,128]{3,2,1,0:T(8,128)(2,1)S(1)}, u32[]{:S(2)}, u32[]{:S(2)}) %collective-permute-start.6) | collective-permute-done | bytes 32800 | tf_op jit(solution)/shard_map/ppermute | solution.py:149
  52.7 4.3 %collective-permute-done.7 = bf16[16,2,8,128]{3,2,1,0:T(8,128)(2,1)S(1)} collective-permute-done((bf16[16,2,8,128]{3,2,1,0:T(8,128)(2,1)S(1)}, bf16[16,2,8,128]{3,2,1,0:T(8,128)(2,1)S(1)}, u32[]{:S(2)}, u32[]{:S(2)}) %collective-permute-start.7) | collective-permute-done | bytes 65568 | tf_op jit(solution)/shard_map/ppermute | solution.py:149
  57.0 6.0 %collective-permute-done.8 = bf16[32,2,8,128]{3,2,1,0:T(8,128)(2,1)S(1)} collective-permute-done((bf16[32,2,8,128]{3,2,1,0:T(8,128)(2,1)S(1)}, bf16[32,2,8,128]{3,2,1,0:T(8,128)(2,1)S(1)}, u32[]{:S(2)}, u32[]{:S(2)}) %collective-permute-start.8) | collective-permute-done | bytes 131104 | tf_op jit(solution)/shard_map/ppermute | solution.py:149
  63.0 0.7 pad_maximum_fusion.1.g_ref
  63.7 18.8 %shard_map.60 = bf16[2,2,4,1024]{3,2,1,0:T(4,128)(2,1)} custom-call(s32[3136]{0:T(1024)} %reshape.348.aper_ref, s32[56]{0:T(128)} %get-tuple-element.29.blk_ref, s32[56]{0:T(128)} %get-tuple-element.28.chk_ref, s32[2]{0:T(128)} %pad_add_fusion.meta_ref, s32[8]{0:T(128)} %copy-done.3, bf16[2,2,8,49,128,128]{5,4,3,2,1,0:T(8,128)(2,1)} %resp_hbm.3, ...), custom_call_target="tpu_custom_call" | custom-call | tf_op jit(solution)/shard_map/pallas_call | solution.py:122
  82.5 0.8 convert_element_type.74
  83.2 4.2 %add_reduce_fusion = (f32[8,4,1024]{2,0,1:T(8,128)S(1)}, f32[8,4,1024]{2,0,1:T(8,128)S(1)}) fusion(f32[2,4,1024]{2,1,0:T(4,128)S(1)} %get-tuple-element.17, f32[2,4,1024]{2,1,0:T(4,128)S(1)} %get-tuple-element.16, f32[2,8]{1,0:T(2,128)S(1)} %get-tuple-element.27, s32[2,8]{1,0:T(2,128)S(1)} %get-tuple-element.25, pred[2,8]{1,0:T(4,128)(4,1)S(1)} %get-tuple-element.23, ...), kind=kLoop, calls=%fused_computation.56 | loop fusion | flops 4915200 | bytes 377120 | tf_op jit(solution)/shard_map/reduce_sum | solution.py:203
  87.5 1.4 %collective-permute-start.9 = (f32[2,2,4,1024]{3,0,2,1:T(2,128)S(1)}, f32[2,2,4,1024]{3,0,2,1:T(2,128)S(1)}, u32[]{:S(2)}, u32[]{:S(2)}) collective-permute-start(f32[2,2,4,1024]{3,0,2,1:T(2,128)S(1)} %get-tuple-element.10), channel_id=1, source_target_pairs={{0,8},{8,16},{16,24},{24,0},{1,9},{9,17},{17,25},{25,1},{2,10},{10... | collective-permute-start | bytes 196616 | tf_op jit(solution)/shard_map/ppermute | solution.py:213
  88.9 1.5 %collective-permute-start.10 = (f32[2,2,4,1024]{3,0,2,1:T(2,128)S(1)}, f32[2,2,4,1024]{3,0,2,1:T(2,128)S(1)}, u32[]{:S(2)}, u32[]{:S(2)}) collective-permute-start(f32[2,2,4,1024]{3,0,2,1:T(2,128)S(1)} %get-tuple-element.11), channel_id=1, source_target_pairs={{0,16},{8,24},{16,0},{24,8},{1,17},{9,25},{17,1},{25,9},{2,18},{10... | collective-permute-start | bytes 196616 | tf_op jit(solution)/shard_map/ppermute | solution.py:213
  91.0 1.8 %collective-permute-done.9 = f32[2,2,4,1024]{3,0,2,1:T(2,128)S(1)} collective-permute-done((f32[2,2,4,1024]{3,0,2,1:T(2,128)S(1)}, f32[2,2,4,1024]{3,0,2,1:T(2,128)S(1)}, u32[]{:S(2)}, u32[]{:S(2)}) %collective-permute-start.9) | collective-permute-done | bytes 65568 | tf_op jit(solution)/shard_map/ppermute | solution.py:213
  92.8 0.7 collective-permute-done.10
  93.4 1.3 %collective-permute-done.11 = f32[2,2,4,1024]{3,0,2,1:T(2,128)S(1)} collective-permute-done((f32[2,2,4,1024]{3,0,2,1:T(2,128)S(1)}, f32[2,2,4,1024]{3,0,2,1:T(2,128)S(1)}, u32[]{:S(2)}, u32[]{:S(2)}) %collective-permute-start.11) | collective-permute-done | bytes 65568 | tf_op jit(solution)/shard_map/ppermute | solution.py:213
  94.8 0.6 copy.14
  (42 shorter events, 2.7 us)
Async XLA Ops:
  0.6 38.9 %copy-start.2 = (s32[4,1024]{1,0:T(4,128)S(1)}, s32[4,1024]{1,0:T(4,128)}, u32[]{:S(2)}) copy-start(s32[4,1024]{1,0:T(4,128)} %param.7) | copy-start | bytes 49156
  1.4 2.4 %collective-permute-start = (bf16[8,2,8,128]{3,2,1,0:T(8,128)(2,1)S(1)}, bf16[8,2,8,128]{3,2,1,0:T(8,128)(2,1)S(1)}, u32[]{:S(2)}, u32[]{:S(2)}) collective-permute-start(bf16[8,2,8,128]{3,2,1,0:T(8,128)(2,1)S(1)} %bitcast.60), channel_id=1, source_target_pairs={{0,1},{1,0},{2,3},{3,2},{4,5},{5,4},{6,7},{7,6},{8,9},{9,8},{10,11... | collective-permute-start | bytes 98312 | tf_op jit(solution)/shard_map/ppermute | solution.py:149
  2.7 17.4 %copy-start.3 = (s32[8]{0:T(128)}, s32[8]{0:T(128)S(1)}, u32[]{:S(2)}) copy-start(s32[8]{0:T(128)S(1)} %convert_reduce_fusion.live_ref) | copy-start | bytes 100
  3.8 4.5 %collective-permute-start.1 = (bf16[16,2,8,128]{3,2,1,0:T(8,128)(2,1)S(1)}, bf16[16,2,8,128]{3,2,1,0:T(8,128)(2,1)S(1)}, u32[]{:S(2)}, u32[]{:S(2)}) collective-permute-start(bf16[16,2,8,128]{3,2,1,0:T(8,128)(2,1)S(1)} %pad_maximum_fusion.4), channel_id=1, source_target_pairs={{0,2},{1,3},{2,0},{3,1},{4,6},{5,7},{6,4},{7,5},{8,10},{9,11},{10,... | collective-permute-start | bytes 196616 | tf_op jit(solution)/shard_map/ppermute | solution.py:149
  8.4 11.0 %collective-permute-start.2 = (bf16[32,2,8,128]{3,2,1,0:T(8,128)(2,1)S(1)}, bf16[32,2,8,128]{3,2,1,0:T(8,128)(2,1)S(1)}, u32[]{:S(2)}, u32[]{:S(2)}) collective-permute-start(bf16[32,2,8,128]{3,2,1,0:T(8,128)(2,1)S(1)} %pad_maximum_fusion.2), channel_id=1, source_target_pairs={{0,4},{1,5},{2,6},{3,7},{4,0},{5,1},{6,2},{7,3},{8,12},{9,13},{10,... | collective-permute-start | bytes 393224 | tf_op jit(solution)/shard_map/ppermute | solution.py:149
  20.1 74.6 %copy-start = (bf16[2,2,4,1024]{3,2,1,0:T(4,128)(2,1)S(1)}, bf16[2,2,4,1024]{3,2,1,0:T(4,128)(2,1)}, u32[]{:S(2)}) copy-start(bf16[2,2,4,1024]{3,2,1,0:T(4,128)(2,1)} %param.6) | copy-start | bytes 98308
  43.8 5.2 %collective-permute-start.3 = (f32[2,2,4,1024]{3,0,2,1:T(2,128)S(1)}, f32[2,2,4,1024]{3,0,2,1:T(2,128)S(1)}, u32[]{:S(2)}, u32[]{:S(2)}) collective-permute-start(f32[2,2,4,1024]{3,0,2,1:T(2,128)S(1)} %get-tuple-element.13), channel_id=1, source_target_pairs={{0,8},{8,16},{16,24},{24,0},{1,9},{9,17},{17,25},{25,1},{2,10},{10... | collective-permute-start | bytes 196616 | tf_op jit(solution)/shard_map/ppermute | solution.py:213
  45.4 4.4 %collective-permute-start.4 = (f32[2,2,4,1024]{3,0,2,1:T(2,128)S(1)}, f32[2,2,4,1024]{3,0,2,1:T(2,128)S(1)}, u32[]{:S(2)}, u32[]{:S(2)}) collective-permute-start(f32[2,2,4,1024]{3,0,2,1:T(2,128)S(1)} %get-tuple-element.14), channel_id=1, source_target_pairs={{0,16},{8,24},{16,0},{24,8},{1,17},{9,25},{17,1},{25,9},{2,18},{10... | collective-permute-start | bytes 196616 | tf_op jit(solution)/shard_map/ppermute | solution.py:213
  46.9 4.3 %collective-permute-start.5 = (f32[2,2,4,1024]{3,0,2,1:T(2,128)S(1)}, f32[2,2,4,1024]{3,0,2,1:T(2,128)S(1)}, u32[]{:S(2)}, u32[]{:S(2)}) collective-permute-start(f32[2,2,4,1024]{3,0,2,1:T(2,128)S(1)} %get-tuple-element.15), channel_id=1, source_target_pairs={{0,24},{8,0},{16,8},{24,16},{1,25},{9,1},{17,9},{25,17},{2,26},{10... | collective-permute-start | bytes 196616 | tf_op jit(solution)/shard_map/ppermute | solution.py:213
  51.2 44.2 %copy-start.1 = (bf16[2,2,4,1024]{3,2,1,0:T(4,128)(2,1)}, bf16[2,2,4,1024]{3,2,1,0:T(4,128)(2,1)S(1)}, u32[]{:S(2)}) copy-start(bf16[2,2,4,1024]{3,2,1,0:T(4,128)(2,1)S(1)} %copy.12) | copy-start | bytes 98308
  51.3 1.3 %collective-permute-start.6 = (bf16[8,2,8,128]{3,2,1,0:T(8,128)(2,1)S(1)}, bf16[8,2,8,128]{3,2,1,0:T(8,128)(2,1)S(1)}, u32[]{:S(2)}, u32[]{:S(2)}) collective-permute-start(bf16[8,2,8,128]{3,2,1,0:T(8,128)(2,1)S(1)} %bitcast.64), channel_id=1, source_target_pairs={{0,1},{1,0},{2,3},{3,2},{4,5},{5,4},{6,7},{7,6},{8,9},{9,8},{10,11... | collective-permute-start | bytes 98312 | tf_op jit(solution)/shard_map/ppermute | solution.py:149
  52.6 4.3 %collective-permute-start.7 = (bf16[16,2,8,128]{3,2,1,0:T(8,128)(2,1)S(1)}, bf16[16,2,8,128]{3,2,1,0:T(8,128)(2,1)S(1)}, u32[]{:S(2)}, u32[]{:S(2)}) collective-permute-start(bf16[16,2,8,128]{3,2,1,0:T(8,128)(2,1)S(1)} %pad_maximum_fusion.5), channel_id=1, source_target_pairs={{0,2},{1,3},{2,0},{3,1},{4,6},{5,7},{6,4},{7,5},{8,10},{9,11},{10,... | collective-permute-start | bytes 196616 | tf_op jit(solution)/shard_map/ppermute | solution.py:149
  56.9 6.0 %collective-permute-start.8 = (bf16[32,2,8,128]{3,2,1,0:T(8,128)(2,1)S(1)}, bf16[32,2,8,128]{3,2,1,0:T(8,128)(2,1)S(1)}, u32[]{:S(2)}, u32[]{:S(2)}) collective-permute-start(bf16[32,2,8,128]{3,2,1,0:T(8,128)(2,1)S(1)} %pad_maximum_fusion.3), channel_id=1, source_target_pairs={{0,4},{1,5},{2,6},{3,7},{4,0},{5,1},{6,2},{7,3},{8,12},{9,13},{10,... | collective-permute-start | bytes 393224 | tf_op jit(solution)/shard_map/ppermute | solution.py:149
  87.5 5.2 %collective-permute-start.9 = (f32[2,2,4,1024]{3,0,2,1:T(2,128)S(1)}, f32[2,2,4,1024]{3,0,2,1:T(2,128)S(1)}, u32[]{:S(2)}, u32[]{:S(2)}) collective-permute-start(f32[2,2,4,1024]{3,0,2,1:T(2,128)S(1)} %get-tuple-element.10), channel_id=1, source_target_pairs={{0,8},{8,16},{16,24},{24,0},{1,9},{9,17},{17,25},{25,1},{2,10},{10... | collective-permute-start | bytes 196616 | tf_op jit(solution)/shard_map/ppermute | solution.py:213
  88.9 4.5 %collective-permute-start.10 = (f32[2,2,4,1024]{3,0,2,1:T(2,128)S(1)}, f32[2,2,4,1024]{3,0,2,1:T(2,128)S(1)}, u32[]{:S(2)}, u32[]{:S(2)}) collective-permute-start(f32[2,2,4,1024]{3,0,2,1:T(2,128)S(1)} %get-tuple-element.11), channel_id=1, source_target_pairs={{0,16},{8,24},{16,0},{24,8},{1,17},{9,25},{17,1},{25,9},{2,18},{10... | collective-permute-start | bytes 196616 | tf_op jit(solution)/shard_map/ppermute | solution.py:213
  90.5 4.3 %collective-permute-start.11 = (f32[2,2,4,1024]{3,0,2,1:T(2,128)S(1)}, f32[2,2,4,1024]{3,0,2,1:T(2,128)S(1)}, u32[]{:S(2)}, u32[]{:S(2)}) collective-permute-start(f32[2,2,4,1024]{3,0,2,1:T(2,128)S(1)} %get-tuple-element.12), channel_id=1, source_target_pairs={{0,24},{8,0},{16,8},{24,16},{1,25},{9,1},{17,9},{25,17},{2,26},{10... | collective-permute-start | bytes 196616 | tf_op jit(solution)/shard_map/ppermute | solution.py:213

commit v4 on v3

--- a/solution.py
+++ b/solution.py
@@ -10,7 +10,7 @@
 NT = 4096
 FBASE = 256
 ITERS = 1
-NBUF = 3
+NBUF = 5
 
 
 def chunk_width(aper_w):

time: 96.6 us -> 92.6 us (0.959)
  Pallas kernels: 37.4 us -> 33 us
    pallas_call x2, Pallas kernels: 37.4 us -> 33 us  [block_products(): pl.pallas_call(kernel, out_shape=jax.ShapeDtypeStruct((freq_dev, 2, focal...]
where the time goes in v4:
time: 92.6 us; the launch traced here: 91 us
  Pallas kernels  33 us (36%)
  waiting for transfers between devices  21.7 us (23%)
  other arithmetic  20.9 us (23%)
  starting transfers between devices  11 us (12%)
  local copies, waits for them, and re-layouts  3.55 us (4%)
    pallas_call x2, Pallas kernels, block_products(): pl.pallas_call(kernel, out_shape=jax.ShapeDtypeStruct((freq_dev, 2, focal...  33 us
    ppermute x6, waiting for transfers between devices, gather_columns(): local = jnp.concatenate([local, lax.ppermute(local, 'rblk', pairs)], axis=0)  15.2 us
    reduce_sum x2, other arithmetic, apply_window(): new_imag = jnp.sum(real_in * c_ri + imag_in * c_ii, axis=0)  8.36 us
    ppermute x6, starting transfers between devices, apply_window(): summed = summed + lax.ppermute(outgoing, 'freq', pairs)  7.98 us
    ppermute x6, waiting for transfers between devices, apply_window(): summed = summed + lax.ppermute(outgoing, 'freq', pairs)  6.56 us
    min x1, other arithmetic, chunk_schedule(): chunks = jnp.clip(entry - starts[blocks], 0, per_blk - 1)  5.6 us
    ppermute x6, starting transfers between devices, gather_columns(): local = jnp.concatenate([local, lax.ppermute(local, 'rblk', pairs)], axis=0)  3.01 us
  transfers between devices with their start and end apart: 12, of which 10 were waited for; matrix products, arithmetic and copies ran while one was open for 12% of the time, Pallas kernels for 0%

profile of v4, /device:TPU:8, one launch (start us, length us, event | category | flops | bytes accessed | tf_op | source)
XLA Modules:
  0.0 91.0 jit_solution(18157996005603340883)
XLA Ops:
  0.6 0.8 reshape.349
  1.8 0.8 compare_select_fusion
  2.9 0.8 fusion.54
  3.9 0.7 fusion.55
  4.6 3.8 %collective-permute-done.1 = bf16[16,2,8,128]{3,2,1,0:T(8,128)(2,1)S(1)} collective-permute-done((bf16[16,2,8,128]{3,2,1,0:T(8,128)(2,1)S(1)}, bf16[16,2,8,128]{3,2,1,0:T(8,128)(2,1)S(1)}, u32[]{:S(2)}, u32[]{:S(2)}) %collective-permute-start.1) | collective-permute-done | bytes 65568 | tf_op jit(solution)/shard_map/ppermute | solution.py:149
  8.4 2.7 %collective-permute-start.2 = (bf16[32,2,8,128]{3,2,1,0:T(8,128)(2,1)S(1)}, bf16[32,2,8,128]{3,2,1,0:T(8,128)(2,1)S(1)}, u32[]{:S(2)}, u32[]{:S(2)}) collective-permute-start(bf16[32,2,8,128]{3,2,1,0:T(8,128)(2,1)S(1)} %pad_maximum_fusion.2), channel_id=1, source_target_pairs={{0,4},{1,5},{2,6},{3,7},{4,0},{5,1},{6,2},{7,3},{8,12},{9,13},{10,... | collective-permute-start | bytes 393224 | tf_op jit(solution)/shard_map/ppermute | solution.py:149
  11.1 5.6 %fusion.53 = (s32[56]{0:T(128)}, s32[56]{0:T(128)}) fusion(s32[]{:T(128)} %bitcast.6, s32[]{:T(128)} %bitcast.7, s32[]{:T(128)} %bitcast.8, s32[]{:T(128)} %bitcast.9, s32[]{:T(128)} %bitcast.10, s32[]{:T(128)} %bitcast.12, s32[]{:T(128)} %bitcast.11, s32[]{:T(128)} %bitcast.5, s32[56]{0:T(128)S(1)} %convert_reduce_fusion.1), kind=kLoop, calls=%fused_computation.148 | loop fusion | flops 1120 | bytes 704 | tf_op jit(solution)/shard_map/jit(clip)/min | solution.py:34
  17.3 0.7 reshape.348.aper_ref
  18.1 1.3 %pad_add_fusion.meta_ref = s32[2]{0:T(128)} fusion(s32[1]{0:T(128)} %bitcast.15, s32[1]{0:T(128)} %bitcast.14), kind=kLoop, calls=%fused_computation.147 | loop fusion | flops 2 | bytes 16 | tf_op jit(solution)/shard_map/stack | solution.py:35
  19.4 0.7 pad_maximum_fusion.g_ref
  20.1 16.4 %shard_map.59 = bf16[2,2,4,1024]{3,2,1,0:T(4,128)(2,1)} custom-call(s32[3136]{0:T(1024)} %reshape.348.aper_ref, s32[56]{0:T(128)} %get-tuple-element.29.blk_ref, s32[56]{0:T(128)} %get-tuple-element.28.chk_ref, s32[2]{0:T(128)} %pad_add_fusion.meta_ref, s32[8]{0:T(128)} %copy-done.3, bf16[2,2,8,49,128,128]{5,4,3,2,1,0:T(8,128)(2,1)} %resp_hbm.3, ...), custom_call_target="tpu_custom_call" | custom-call | tf_op jit(solution)/shard_map/pallas_call | solution.py:122
  36.5 0.8 convert_element_type.72
  37.3 4.2 %add_reduce_fusion.2 = (f32[8,4,1024]{2,0,1:T(8,128)S(1)}, f32[8,4,1024]{2,0,1:T(8,128)S(1)}) fusion(f32[2,4,1024]{2,1,0:T(4,128)S(1)} %get-tuple-element.19, f32[2,4,1024]{2,1,0:T(4,128)S(1)} %get-tuple-element.18, f32[2,8]{1,0:T(2,128)S(1)} %get-tuple-element.27, s32[2,8]{1,0:T(2,128)S(1)} %get-tuple-element.25, pred[2,8]{1,0:T(4,128)(4,1)S(1)} %get-tuple-element.23, ...), kind=kLoop, calls=%fused_computation.58 | loop fusion | flops 4915200 | bytes 377120 | tf_op jit(solution)/shard_map/reduce_sum | solution.py:203
  41.6 1.5 %collective-permute-start.3 = (f32[2,2,4,1024]{3,0,2,1:T(2,128)S(1)}, f32[2,2,4,1024]{3,0,2,1:T(2,128)S(1)}, u32[]{:S(2)}, u32[]{:S(2)}) collective-permute-start(f32[2,2,4,1024]{3,0,2,1:T(2,128)S(1)} %get-tuple-element.13), channel_id=1, source_target_pairs={{0,8},{8,16},{16,24},{24,0},{1,9},{9,17},{17,25},{25,1},{2,10},{10... | collective-permute-start | bytes 196616 | tf_op jit(solution)/shard_map/ppermute | solution.py:213
  43.2 1.5 %collective-permute-start.4 = (f32[2,2,4,1024]{3,0,2,1:T(2,128)S(1)}, f32[2,2,4,1024]{3,0,2,1:T(2,128)S(1)}, u32[]{:S(2)}, u32[]{:S(2)}) collective-permute-start(f32[2,2,4,1024]{3,0,2,1:T(2,128)S(1)} %get-tuple-element.14), channel_id=1, source_target_pairs={{0,16},{8,24},{16,0},{24,8},{1,17},{9,25},{17,1},{25,9},{2,18},{10... | collective-permute-start | bytes 196616 | tf_op jit(solution)/shard_map/ppermute | solution.py:213
  44.7 1.4 %collective-permute-start.5 = (f32[2,2,4,1024]{3,0,2,1:T(2,128)S(1)}, f32[2,2,4,1024]{3,0,2,1:T(2,128)S(1)}, u32[]{:S(2)}, u32[]{:S(2)}) collective-permute-start(f32[2,2,4,1024]{3,0,2,1:T(2,128)S(1)} %get-tuple-element.15), channel_id=1, source_target_pairs={{0,24},{8,0},{16,8},{24,16},{1,25},{9,1},{17,9},{25,17},{2,26},{10... | collective-permute-start | bytes 196616 | tf_op jit(solution)/shard_map/ppermute | solution.py:213
  46.1 0.7 collective-permute-done.3
  46.8 0.7 collective-permute-done.4
  47.5 1.4 %collective-permute-done.5 = f32[2,2,4,1024]{3,0,2,1:T(2,128)S(1)} collective-permute-done((f32[2,2,4,1024]{3,0,2,1:T(2,128)S(1)}, f32[2,2,4,1024]{3,0,2,1:T(2,128)S(1)}, u32[]{:S(2)}, u32[]{:S(2)}) %collective-permute-start.5) | collective-permute-done | bytes 65568 | tf_op jit(solution)/shard_map/ppermute | solution.py:213
  49.2 1.2 %collective-permute-done.6 = bf16[8,2,8,128]{3,2,1,0:T(8,128)(2,1)S(1)} collective-permute-done((bf16[8,2,8,128]{3,2,1,0:T(8,128)(2,1)S(1)}, bf16[8,2,8,128]{3,2,1,0:T(8,128)(2,1)S(1)}, u32[]{:S(2)}, u32[]{:S(2)}) %collective-permute-start.6) | collective-permute-done | bytes 32800 | tf_op jit(solution)/shard_map/ppermute | solution.py:149
  50.4 4.3 %collective-permute-done.7 = bf16[16,2,8,128]{3,2,1,0:T(8,128)(2,1)S(1)} collective-permute-done((bf16[16,2,8,128]{3,2,1,0:T(8,128)(2,1)S(1)}, bf16[16,2,8,128]{3,2,1,0:T(8,128)(2,1)S(1)}, u32[]{:S(2)}, u32[]{:S(2)}) %collective-permute-start.7) | collective-permute-done | bytes 65568 | tf_op jit(solution)/shard_map/ppermute | solution.py:149
  54.8 6.0 %collective-permute-done.8 = bf16[32,2,8,128]{3,2,1,0:T(8,128)(2,1)S(1)} collective-permute-done((bf16[32,2,8,128]{3,2,1,0:T(8,128)(2,1)S(1)}, bf16[32,2,8,128]{3,2,1,0:T(8,128)(2,1)S(1)}, u32[]{:S(2)}, u32[]{:S(2)}) %collective-permute-start.8) | collective-permute-done | bytes 131104 | tf_op jit(solution)/shard_map/ppermute | solution.py:149
  60.8 0.7 pad_maximum_fusion.1.g_ref
  61.5 16.5 %shard_map.60 = bf16[2,2,4,1024]{3,2,1,0:T(4,128)(2,1)} custom-call(s32[3136]{0:T(1024)} %reshape.348.aper_ref, s32[56]{0:T(128)} %get-tuple-element.29.blk_ref, s32[56]{0:T(128)} %get-tuple-element.28.chk_ref, s32[2]{0:T(128)} %pad_add_fusion.meta_ref, s32[8]{0:T(128)} %copy-done.3, bf16[2,2,8,49,128,128]{5,4,3,2,1,0:T(8,128)(2,1)} %resp_hbm.3, ...), custom_call_target="tpu_custom_call" | custom-call | tf_op jit(solution)/shard_map/pallas_call | solution.py:122
  78.0 0.8 convert_element_type.74
  78.8 4.2 %add_reduce_fusion = (f32[8,4,1024]{2,0,1:T(8,128)S(1)}, f32[8,4,1024]{2,0,1:T(8,128)S(1)}) fusion(f32[2,4,1024]{2,1,0:T(4,128)S(1)} %get-tuple-element.17, f32[2,4,1024]{2,1,0:T(4,128)S(1)} %get-tuple-element.16, f32[2,8]{1,0:T(2,128)S(1)} %get-tuple-element.27, s32[2,8]{1,0:T(2,128)S(1)} %get-tuple-element.25, pred[2,8]{1,0:T(4,128)(4,1)S(1)} %get-tuple-element.23, ...), kind=kLoop, calls=%fused_computation.56 | loop fusion | flops 4915200 | bytes 377120 | tf_op jit(solution)/shard_map/reduce_sum | solution.py:203
  83.1 1.4 %collective-permute-start.9 = (f32[2,2,4,1024]{3,0,2,1:T(2,128)S(1)}, f32[2,2,4,1024]{3,0,2,1:T(2,128)S(1)}, u32[]{:S(2)}, u32[]{:S(2)}) collective-permute-start(f32[2,2,4,1024]{3,0,2,1:T(2,128)S(1)} %get-tuple-element.10), channel_id=1, source_target_pairs={{0,8},{8,16},{16,24},{24,0},{1,9},{9,17},{17,25},{25,1},{2,10},{10... | collective-permute-start | bytes 196616 | tf_op jit(solution)/shard_map/ppermute | solution.py:213
  84.5 1.5 %collective-permute-start.10 = (f32[2,2,4,1024]{3,0,2,1:T(2,128)S(1)}, f32[2,2,4,1024]{3,0,2,1:T(2,128)S(1)}, u32[]{:S(2)}, u32[]{:S(2)}) collective-permute-start(f32[2,2,4,1024]{3,0,2,1:T(2,128)S(1)} %get-tuple-element.11), channel_id=1, source_target_pairs={{0,16},{8,24},{16,0},{24,8},{1,17},{9,25},{17,1},{25,9},{2,18},{10... | collective-permute-start | bytes 196616 | tf_op jit(solution)/shard_map/ppermute | solution.py:213
  86.6 1.8 %collective-permute-done.9 = f32[2,2,4,1024]{3,0,2,1:T(2,128)S(1)} collective-permute-done((f32[2,2,4,1024]{3,0,2,1:T(2,128)S(1)}, f32[2,2,4,1024]{3,0,2,1:T(2,128)S(1)}, u32[]{:S(2)}, u32[]{:S(2)}) %collective-permute-start.9) | collective-permute-done | bytes 65568 | tf_op jit(solution)/shard_map/ppermute | solution.py:213
  88.3 0.7 collective-permute-done.10
  89.0 1.3 %collective-permute-done.11 = f32[2,2,4,1024]{3,0,2,1:T(2,128)S(1)} collective-permute-done((f32[2,2,4,1024]{3,0,2,1:T(2,128)S(1)}, f32[2,2,4,1024]{3,0,2,1:T(2,128)S(1)}, u32[]{:S(2)}, u32[]{:S(2)}) %collective-permute-start.11) | collective-permute-done | bytes 65568 | tf_op jit(solution)/shard_map/ppermute | solution.py:213
  90.4 0.6 copy.14
  (42 shorter events, 2.7 us)
Async XLA Ops:
  0.6 36.7 %copy-start.2 = (s32[4,1024]{1,0:T(4,128)S(1)}, s32[4,1024]{1,0:T(4,128)}, u32[]{:S(2)}) copy-start(s32[4,1024]{1,0:T(4,128)} %param.7) | copy-start | bytes 49156
  1.4 2.4 %collective-permute-start = (bf16[8,2,8,128]{3,2,1,0:T(8,128)(2,1)S(1)}, bf16[8,2,8,128]{3,2,1,0:T(8,128)(2,1)S(1)}, u32[]{:S(2)}, u32[]{:S(2)}) collective-permute-start(bf16[8,2,8,128]{3,2,1,0:T(8,128)(2,1)S(1)} %bitcast.60), channel_id=1, source_target_pairs={{0,1},{1,0},{2,3},{3,2},{4,5},{5,4},{6,7},{7,6},{8,9},{9,8},{10,11... | collective-permute-start | bytes 98312 | tf_op jit(solution)/shard_map/ppermute | solution.py:149
  2.7 17.4 %copy-start.3 = (s32[8]{0:T(128)}, s32[8]{0:T(128)S(1)}, u32[]{:S(2)}) copy-start(s32[8]{0:T(128)S(1)} %convert_reduce_fusion.live_ref) | copy-start | bytes 100
  3.8 4.5 %collective-permute-start.1 = (bf16[16,2,8,128]{3,2,1,0:T(8,128)(2,1)S(1)}, bf16[16,2,8,128]{3,2,1,0:T(8,128)(2,1)S(1)}, u32[]{:S(2)}, u32[]{:S(2)}) collective-permute-start(bf16[16,2,8,128]{3,2,1,0:T(8,128)(2,1)S(1)} %pad_maximum_fusion.4), channel_id=1, source_target_pairs={{0,2},{1,3},{2,0},{3,1},{4,6},{5,7},{6,4},{7,5},{8,10},{9,11},{10,... | collective-permute-start | bytes 196616 | tf_op jit(solution)/shard_map/ppermute | solution.py:149
  8.4 11.0 %collective-permute-start.2 = (bf16[32,2,8,128]{3,2,1,0:T(8,128)(2,1)S(1)}, bf16[32,2,8,128]{3,2,1,0:T(8,128)(2,1)S(1)}, u32[]{:S(2)}, u32[]{:S(2)}) collective-permute-start(bf16[32,2,8,128]{3,2,1,0:T(8,128)(2,1)S(1)} %pad_maximum_fusion.2), channel_id=1, source_target_pairs={{0,4},{1,5},{2,6},{3,7},{4,0},{5,1},{6,2},{7,3},{8,12},{9,13},{10,... | collective-permute-start | bytes 393224 | tf_op jit(solution)/shard_map/ppermute | solution.py:149
  20.1 70.2 %copy-start = (bf16[2,2,4,1024]{3,2,1,0:T(4,128)(2,1)S(1)}, bf16[2,2,4,1024]{3,2,1,0:T(4,128)(2,1)}, u32[]{:S(2)}) copy-start(bf16[2,2,4,1024]{3,2,1,0:T(4,128)(2,1)} %param.6) | copy-start | bytes 98308
  41.6 5.2 %collective-permute-start.3 = (f32[2,2,4,1024]{3,0,2,1:T(2,128)S(1)}, f32[2,2,4,1024]{3,0,2,1:T(2,128)S(1)}, u32[]{:S(2)}, u32[]{:S(2)}) collective-permute-start(f32[2,2,4,1024]{3,0,2,1:T(2,128)S(1)} %get-tuple-element.13), channel_id=1, source_target_pairs={{0,8},{8,16},{16,24},{24,0},{1,9},{9,17},{17,25},{25,1},{2,10},{10... | collective-permute-start | bytes 196616 | tf_op jit(solution)/shard_map/ppermute | solution.py:213
  43.2 4.4 %collective-permute-start.4 = (f32[2,2,4,1024]{3,0,2,1:T(2,128)S(1)}, f32[2,2,4,1024]{3,0,2,1:T(2,128)S(1)}, u32[]{:S(2)}, u32[]{:S(2)}) collective-permute-start(f32[2,2,4,1024]{3,0,2,1:T(2,128)S(1)} %get-tuple-element.14), channel_id=1, source_target_pairs={{0,16},{8,24},{16,0},{24,8},{1,17},{9,25},{17,1},{25,9},{2,18},{10... | collective-permute-start | bytes 196616 | tf_op jit(solution)/shard_map/ppermute | solution.py:213
  44.7 4.3 %collective-permute-start.5 = (f32[2,2,4,1024]{3,0,2,1:T(2,128)S(1)}, f32[2,2,4,1024]{3,0,2,1:T(2,128)S(1)}, u32[]{:S(2)}, u32[]{:S(2)}) collective-permute-start(f32[2,2,4,1024]{3,0,2,1:T(2,128)S(1)} %get-tuple-element.15), channel_id=1, source_target_pairs={{0,24},{8,0},{16,8},{24,16},{1,25},{9,1},{17,9},{25,17},{2,26},{10... | collective-permute-start | bytes 196616 | tf_op jit(solution)/shard_map/ppermute | solution.py:213
  49.0 42.0 %copy-start.1 = (bf16[2,2,4,1024]{3,2,1,0:T(4,128)(2,1)}, bf16[2,2,4,1024]{3,2,1,0:T(4,128)(2,1)S(1)}, u32[]{:S(2)}) copy-start(bf16[2,2,4,1024]{3,2,1,0:T(4,128)(2,1)S(1)} %copy.12) | copy-start | bytes 98308
  49.1 1.3 %collective-permute-start.6 = (bf16[8,2,8,128]{3,2,1,0:T(8,128)(2,1)S(1)}, bf16[8,2,8,128]{3,2,1,0:T(8,128)(2,1)S(1)}, u32[]{:S(2)}, u32[]{:S(2)}) collective-permute-start(bf16[8,2,8,128]{3,2,1,0:T(8,128)(2,1)S(1)} %bitcast.64), channel_id=1, source_target_pairs={{0,1},{1,0},{2,3},{3,2},{4,5},{5,4},{6,7},{7,6},{8,9},{9,8},{10,11... | collective-permute-start | bytes 98312 | tf_op jit(solution)/shard_map/ppermute | solution.py:149
  50.4 4.3 %collective-permute-start.7 = (bf16[16,2,8,128]{3,2,1,0:T(8,128)(2,1)S(1)}, bf16[16,2,8,128]{3,2,1,0:T(8,128)(2,1)S(1)}, u32[]{:S(2)}, u32[]{:S(2)}) collective-permute-start(bf16[16,2,8,128]{3,2,1,0:T(8,128)(2,1)S(1)} %pad_maximum_fusion.5), channel_id=1, source_target_pairs={{0,2},{1,3},{2,0},{3,1},{4,6},{5,7},{6,4},{7,5},{8,10},{9,11},{10,... | collective-permute-start | bytes 196616 | tf_op jit(solution)/shard_map/ppermute | solution.py:149
  54.7 6.0 %collective-permute-start.8 = (bf16[32,2,8,128]{3,2,1,0:T(8,128)(2,1)S(1)}, bf16[32,2,8,128]{3,2,1,0:T(8,128)(2,1)S(1)}, u32[]{:S(2)}, u32[]{:S(2)}) collective-permute-start(bf16[32,2,8,128]{3,2,1,0:T(8,128)(2,1)S(1)} %pad_maximum_fusion.3), channel_id=1, source_target_pairs={{0,4},{1,5},{2,6},{3,7},{4,0},{5,1},{6,2},{7,3},{8,12},{9,13},{10,... | collective-permute-start | bytes 393224 | tf_op jit(solution)/shard_map/ppermute | solution.py:149
  83.1 5.2 %collective-permute-start.9 = (f32[2,2,4,1024]{3,0,2,1:T(2,128)S(1)}, f32[2,2,4,1024]{3,0,2,1:T(2,128)S(1)}, u32[]{:S(2)}, u32[]{:S(2)}) collective-permute-start(f32[2,2,4,1024]{3,0,2,1:T(2,128)S(1)} %get-tuple-element.10), channel_id=1, source_target_pairs={{0,8},{8,16},{16,24},{24,0},{1,9},{9,17},{17,25},{25,1},{2,10},{10... | collective-permute-start | bytes 196616 | tf_op jit(solution)/shard_map/ppermute | solution.py:213
  84.5 4.5 %collective-permute-start.10 = (f32[2,2,4,1024]{3,0,2,1:T(2,128)S(1)}, f32[2,2,4,1024]{3,0,2,1:T(2,128)S(1)}, u32[]{:S(2)}, u32[]{:S(2)}) collective-permute-start(f32[2,2,4,1024]{3,0,2,1:T(2,128)S(1)} %get-tuple-element.11), channel_id=1, source_target_pairs={{0,16},{8,24},{16,0},{24,8},{1,17},{9,25},{17,1},{25,9},{2,18},{10... | collective-permute-start | bytes 196616 | tf_op jit(solution)/shard_map/ppermute | solution.py:213
  86.0 4.3 %collective-permute-start.11 = (f32[2,2,4,1024]{3,0,2,1:T(2,128)S(1)}, f32[2,2,4,1024]{3,0,2,1:T(2,128)S(1)}, u32[]{:S(2)}, u32[]{:S(2)}) collective-permute-start(f32[2,2,4,1024]{3,0,2,1:T(2,128)S(1)} %get-tuple-element.12), channel_id=1, source_target_pairs={{0,24},{8,0},{16,8},{24,16},{1,25},{9,1},{17,9},{25,17},{2,26},{10... | collective-permute-start | bytes 196616 | tf_op jit(solution)/shard_map/ppermute | solution.py:213

commit v5 on v4

--- a/solution.py
+++ b/solution.py
@@ -10,6 +10,7 @@
 NT = 4096
 FBASE = 256
 ITERS = 1
+BLOCK = 128
 NBUF = 5
 
 
@@ -36,16 +37,18 @@
     return blocks, chunks, meta, live
 
 
-def block_products(gathered, response, aperture, first_block, conjugate):
+def block_products(gathered, response, aperture, first_block, tables, conjugate):
     freq_dev, unused, blk_dev, aper_w, block_rows, block_cols = response.shape
     rows_g = gathered.shape[2]
     chunk = chunk_width(aper_w)
     blocks, chunks, meta, live = chunk_schedule(aperture, first_block, blk_dev, chunk)
     flat_aperture = aperture.reshape(-1)
     focal = rows_g // 2
-
-    def kernel(aper_ref, blk_ref, chk_ref, meta_ref, live_ref, resp_hbm, g_ref, out_ref,
-               buf, sem, pcat, acc):
+    freq_all = tables[0].shape[0] - freq_dev + 1
+    scale = 1.0 / NT
+
+    def kernel(aper_ref, blk_ref, chk_ref, meta_ref, live_ref, resp_hbm, g_ref,
+               near_re_ref, near_im_ref, far_re_ref, far_im_ref, out_ref, buf, sem, pcat, acc):
         first = meta_ref[0]
         total = meta_ref[1]
         acc[...] = jnp.zeros(acc.shape, jnp.float32)
@@ -101,6 +104,8 @@
         lax.fori_loop(0, total, body, 0)
 
         for b in range(blk_dev):
+            cols = pl.ds(b * block_rows, block_rows)
+            parts = []
             for f in range(freq_dev):
                 v = acc[b, f].T
                 p00 = v[0:focal, 0:block_rows]
@@ -113,18 +118,36 @@
                 else:
                     real_part = p00 - p11
                     imag_part = p10 + p01
-                cols = pl.ds(b * block_rows, block_rows)
-                out_ref[f, 0, :, cols] = real_part.astype(out_ref.dtype)
-                out_ref[f, 1, :, cols] = imag_part.astype(out_ref.dtype)
+                parts.append((
+                    real_part.astype(jnp.bfloat16).astype(jnp.float32),
+                    imag_part.astype(jnp.bfloat16).astype(jnp.float32),
+                ))
+            for l in range(freq_all):
+                new_real = None
+                new_imag = None
+                for f, (real_in, imag_in) in enumerate(parts):
+                    near_at = f - l + freq_all - 1
+                    far_at = f + l
+                    rows = pl.ds(b * focal, focal)
+                    near_re = near_re_ref[near_at, rows, :]
+                    near_im = near_im_ref[near_at, rows, :]
+                    far_re = far_re_ref[far_at, rows, :]
+                    far_im = far_im_ref[far_at, rows, :]
+                    term_real = real_in * (near_re + far_re) + imag_in * (far_im - near_im)
+                    term_imag = real_in * (near_im + far_im) + imag_in * (near_re - far_re)
+                    new_real = term_real if new_real is None else new_real + term_real
+                    new_imag = term_imag if new_imag is None else new_imag + term_imag
+                out_ref[l, 0, :, cols] = new_real * scale
+                out_ref[l, 1, :, cols] = new_imag * scale
 
     smem = pl.BlockSpec(memory_space=pltpu.SMEM)
     vmem = pl.BlockSpec(memory_space=pltpu.VMEM)
     return pl.pallas_call(
         kernel,
         out_shape=jax.ShapeDtypeStruct(
-            (freq_dev, 2, focal, blk_dev * block_rows), jnp.bfloat16
+            (freq_all, 2, focal, blk_dev * block_rows), jnp.float32
         ),
-        in_specs=[smem, smem, smem, smem, smem, pl.BlockSpec(memory_space=pl.ANY), vmem],
+        in_specs=[smem] * 5 + [pl.BlockSpec(memory_space=pl.ANY)] + [vmem] * 5,
         out_specs=vmem,
         scratch_shapes=[
             pltpu.VMEM((NBUF, freq_dev, 2, block_rows, chunk * block_cols), response.dtype),
@@ -132,7 +155,7 @@
             pltpu.VMEM((freq_dev, rows_g, chunk * block_cols), response.dtype),
             pltpu.VMEM((blk_dev, freq_dev, 2 * block_rows, rows_g), jnp.float32),
         ],
-    )(flat_aperture, blocks, chunks, meta, live, response, gathered)
+    )(flat_aperture, blocks, chunks, meta, live, response, gathered, *tables)
 
 
 def gather_columns(spectra, block_rows):
@@ -180,29 +203,19 @@
 
 def window_tables(arrival, freq_dev, freq_all):
     first = lax.axis_index("freq") * freq_dev
-    mine = FBASE + first + jnp.arange(freq_dev, dtype=jnp.int32)
-    every = FBASE + jnp.arange(freq_all, dtype=jnp.int32)
-    limits = arrival[None, None]
-    near_re, near_im = dirichlet((mine[:, None] - every[None, :])[:, :, None, None], limits)
-    far_re, far_im = dirichlet((-(mine[:, None] + every[None, :]))[:, :, None, None], limits)
-    scale = jnp.float32(1.0 / NT)
-    return (
-        (near_re + far_re) * scale,
-        (far_im - near_im) * scale,
-        (near_im + far_im) * scale,
-        (near_re - far_re) * scale,
-    )
-
-
-def apply_window(spectra, tables):
-    c_rr, c_ir, c_ri, c_ii = tables
-    values = spectra.astype(jnp.float32)
-    real_in = values[:, 0][:, None]
-    imag_in = values[:, 1][:, None]
-    new_real = jnp.sum(real_in * c_rr + imag_in * c_ir, axis=0)
-    new_imag = jnp.sum(real_in * c_ri + imag_in * c_ii, axis=0)
-    partial = jnp.stack([new_real, new_imag], axis=1)
-    freq_dev = spectra.shape[0]
+    steps = jnp.arange(freq_dev + freq_all - 1, dtype=jnp.int32)
+    focal, traces = arrival.shape
+    blocks = traces // BLOCK
+    dense = jnp.transpose(arrival.reshape(focal, blocks, BLOCK), (1, 0, 2))
+    limits = dense.reshape(blocks * focal, BLOCK)[None]
+    near_offsets = first - (freq_all - 1) + steps
+    far_offsets = -(2 * FBASE + first + steps)
+    near_re, near_im = dirichlet(near_offsets[:, None, None], limits)
+    far_re, far_im = dirichlet(far_offsets[:, None, None], limits)
+    return near_re, near_im, far_re, far_im
+
+
+def reduce_window(partial, freq_dev):
     count = lax.axis_size("freq")
     me = lax.axis_index("freq")
     summed = lax.dynamic_slice_in_dim(partial, me * freq_dev, freq_dev, 0)
@@ -226,11 +239,11 @@
     window_q = focus_init
     for iteration in range(ITERS):
         gathered = gather_columns(current, block_rows)
-        forward = block_products(gathered, response, ordered, first_block, False)
-        window_q = apply_window(forward, tables)
+        forward = block_products(gathered, response, ordered, first_block, tables, False)
+        window_q = reduce_window(forward, freq_dev)
         mirrored = gather_columns(window_q, block_rows)
-        adjoint = block_products(mirrored, response, ordered, first_block, True)
-        windowed = apply_window(adjoint, tables)
+        adjoint = block_products(mirrored, response, ordered, first_block, tables, True)
+        windowed = reduce_window(adjoint, freq_dev)
         current = (focus_init.astype(jnp.float32) + windowed.astype(jnp.float32)).astype(
             jnp.bfloat16
         )

time: 92.6 us -> 87.7 us (0.947); the launches traced: 91 us -> 88.1 us
  other arithmetic: 20.9 us -> 15.2 us
  local copies, waits for them, and re-layouts: 3.55 us -> 5.57 us
  starting transfers between devices: 11 us -> 12 us
  waiting for transfers between devices: 21.7 us -> 20.7 us
    reduce_sum x2 -> x0, other arithmetic: 8.36 us -> none  [apply_window(): new_imag = jnp.sum(real_in * c_ri + imag_in * c_ii, axis=0)]
    mul x2 -> x1, other arithmetic: 0.03 us -> 3.24 us  [dirichlet(): return (ratio * jnp.cos(angle), ratio * jnp.sin(angle))]
    dynamic_slice x0 -> x2, local copies, waits for them, and re-layouts: none -> 1.85 us  [reduce_window(): outgoing = lax.dynamic_slice_in_dim(partial, target * freq_dev, freq_dev, 0)]
    convert_element_type x1, other arithmetic: 0.09 us -> 1.5 us  [shards(): (focus_init.astype(jnp.float32) + windowed.astype(jnp.float32)).astype(jn...]
    ppermute x6, waiting for transfers between devices: 6.56 us -> 5.49 us  [reduce_window(): summed = summed + lax.ppermute(outgoing, 'freq', pairs)]
    ppermute x6, starting transfers between devices: 7.98 us -> 8.99 us  [reduce_window(): summed = summed + lax.ppermute(outgoing, 'freq', pairs)]
  transfers between devices with their start and end apart: 12 -> 12, of which waited for: 10 -> 10; matrix products, arithmetic and copies ran while one was open for 12% -> 16% of each run, Pallas kernels for 0% -> 0%
where the time goes in v5:
time: 87.7 us; the launch traced here: 88.1 us
  Pallas kernels  33.8 us (39%)
  waiting for transfers between devices  20.7 us (24%)
  other arithmetic  15.2 us (17%)
  starting transfers between devices  12 us (14%)
  local copies, waits for them, and re-layouts  5.57 us (6%)
    pallas_call x2, Pallas kernels, block_products(): pl.pallas_call(kernel, out_shape=jax.ShapeDtypeStruct((freq_all, 2, focal...  33.8 us
    ppermute x6, waiting for transfers between devices, gather_columns(): local = jnp.concatenate([local, lax.ppermute(local, 'rblk', pairs)], axis=0)  15.2 us
    ppermute x6, starting transfers between devices, reduce_window(): summed = summed + lax.ppermute(outgoing, 'freq', pairs)  8.99 us
    min x1, other arithmetic, chunk_schedule(): chunks = jnp.clip(entry - starts[blocks], 0, per_blk - 1)  5.59 us
    ppermute x6, waiting for transfers between devices, reduce_window(): summed = summed + lax.ppermute(outgoing, 'freq', pairs)  5.49 us
    mul x1, other arithmetic, dirichlet(): return (ratio * jnp.cos(angle), ratio * jnp.sin(angle))  3.24 us
    ppermute x6, starting transfers between devices, gather_columns(): local = jnp.concatenate([local, lax.ppermute(local, 'rblk', pairs)], axis=0)  3.01 us
    dynamic_slice x2, local copies, waits for them, and re-layouts, reduce_window(): outgoing = lax.dynamic_slice_in_dim(partial, target * freq_dev, freq_dev, 0)  1.85 us
  transfers between devices with their start and end apart: 12, of which 10 were waited for; matrix products, arithmetic and copies ran while one was open for 16% of the time, Pallas kernels for 0%

profile of v5, /device:TPU:8, one launch (start us, length us, event | category | flops | bytes accessed | tf_op | source)
XLA Modules:
  0.0 88.1 jit_solution(17818677147653104002)
XLA Ops:
  0.6 0.8 reshape.204
  1.6 0.7 copy.21
  2.4 0.8 compare_select_fusion
  3.5 3.2 %sine_multiply_fusion = (f32[9,32,128]{2,1,0:T(8,128)}, f32[9,32,128]{2,1,0:T(8,128)}, f32[9,32,128]{2,1,0:T(8,128)}, f32[9,32,128]{2,1,0:T(8,128)}) fusion(s32[9]{0:T(128)S(1)} %get-tuple-element.30, s32[32,128]{1,0:T(8,128)S(1)} %broadcast_add_fusion, f32[9]{0:T(128)S(1)} %get-tuple-element.29, s32[32,128]{1,0:T(8,128)S(1)} %bitcast.58, ...), kind=kLoop, calls=%fused_computation.40 | loop fusion | flops 2359296 | bytes 639138 | tf_op jit(solution)/shard_map/mul | solution.py:201
  7.6 3.8 %collective-permute-done.1 = bf16[16,2,8,128]{3,2,1,0:T(8,128)(2,1)S(1)} collective-permute-done((bf16[16,2,8,128]{3,2,1,0:T(8,128)(2,1)S(1)}, bf16[16,2,8,128]{3,2,1,0:T(8,128)(2,1)S(1)}, u32[]{:S(2)}, u32[]{:S(2)}) %collective-permute-start.1) | collective-permute-done | bytes 65568 | tf_op jit(solution)/shard_map/ppermute | solution.py:172
  11.4 2.7 %collective-permute-start.2 = (bf16[32,2,8,128]{3,2,1,0:T(8,128)(2,1)S(1)}, bf16[32,2,8,128]{3,2,1,0:T(8,128)(2,1)S(1)}, u32[]{:S(2)}, u32[]{:S(2)}) collective-permute-start(bf16[32,2,8,128]{3,2,1,0:T(8,128)(2,1)S(1)} %pad_maximum_fusion.2), channel_id=1, source_target_pairs={{0,4},{1,5},{2,6},{3,7},{4,0},{5,1},{6,2},{7,3},{8,12},{9,13},{10,... | collective-permute-start | bytes 393224 | tf_op jit(solution)/shard_map/ppermute | solution.py:172
  14.0 5.6 %fusion.38 = (s32[56]{0:T(128)}, s32[56]{0:T(128)}) fusion(s32[]{:T(128)} %bitcast.6, s32[]{:T(128)} %bitcast.7, s32[]{:T(128)} %bitcast.8, s32[]{:T(128)} %bitcast.9, s32[]{:T(128)} %bitcast.10, s32[]{:T(128)} %bitcast.12, s32[]{:T(128)} %bitcast.11, s32[]{:T(128)} %bitcast.5, s32[56]{0:T(128)S(1)} %convert_reduce_fusion.1), kind=kLoop, calls=%fused_computation.116 | loop fusion | flops 1120 | bytes 704 | tf_op jit(solution)/shard_map/jit(clip)/min | solution.py:35
  20.3 0.7 reshape.203.aper_ref
  21.1 1.3 %pad_add_fusion.meta_ref = s32[2]{0:T(128)} fusion(s32[1]{0:T(128)} %bitcast.15, s32[1]{0:T(128)} %bitcast.14), kind=kLoop, calls=%fused_computation.112 | loop fusion | flops 2 | bytes 16 | tf_op jit(solution)/shard_map/stack | solution.py:36
  22.4 0.7 pad_maximum_fusion.g_ref
  23.1 16.9 %shard_map.59 = f32[8,2,4,1024]{3,2,1,0:T(4,128)} custom-call(s32[3136]{0:T(1024)} %reshape.203.aper_ref, s32[56]{0:T(128)} %get-tuple-element.17.blk_ref, s32[56]{0:T(128)} %get-tuple-element.16.chk_ref, s32[2]{0:T(128)} %pad_add_fusion.meta_ref, s32[8]{0:T(128)} %copy-done.2, bf16[2,2,8,49,128,128]{5,4,3,2,1,0:T(8,128)(2,1)} %resp_hbm.3, ...), custom_call_target="tpu_custom_call" | custom-call | tf_op jit(solution)/shard_map/pallas_call | solution.py:145
  40.0 0.9 %constant_dynamic-slice_fusion.5 = (f32[2,2,4,1024]{3,2,1,0:T(4,128)S(1)}, f32[2,2,4,1024]{3,2,1,0:T(4,128)S(1)}, f32[2,2,4,1024]{3,2,1,0:T(4,128)S(1)}) fusion(f32[8,2,4,1024]{3,2,1,0:T(4,128)} %shard_map.59, s32[]{:T(128)S(6)} %select_n.188, s32[]{:T(128)S(6)} %select_n.192, s32[]{:T(128)S(6)} %select_n.190), kind=kLoop, calls=%fused_computation.78 | loop fusion | bytes 393228 | tf_op jit(solution)/shard_map/dynamic_slice | solution.py:224
  40.9 1.5 %collective-permute-start.3 = (f32[2,2,4,1024]{3,2,1,0:T(4,128)S(1)}, f32[2,2,4,1024]{3,2,1,0:T(4,128)S(1)}, u32[]{:S(2)}, u32[]{:S(2)}) collective-permute-start(f32[2,2,4,1024]{3,2,1,0:T(4,128)S(1)} %get-tuple-element.7), channel_id=1, source_target_pairs={{0,8},{8,16},{16,24},{24,0},{1,9},{9,17},{17,25},{25,1},{2,10},{10... | collective-permute-start | bytes 196616 | tf_op jit(solution)/shard_map/ppermute | solution.py:226
  42.5 1.4 %collective-permute-start.5 = (f32[2,2,4,1024]{3,2,1,0:T(4,128)S(1)}, f32[2,2,4,1024]{3,2,1,0:T(4,128)S(1)}, u32[]{:S(2)}, u32[]{:S(2)}) collective-permute-start(f32[2,2,4,1024]{3,2,1,0:T(4,128)S(1)} %get-tuple-element.8), channel_id=1, source_target_pairs={{0,24},{8,0},{16,8},{24,16},{1,25},{9,1},{17,9},{25,17},{2,26},{10... | collective-permute-start | bytes 196616 | tf_op jit(solution)/shard_map/ppermute | solution.py:226
  43.9 1.5 %collective-permute-start.4 = (f32[2,2,4,1024]{3,2,1,0:T(4,128)S(1)}, f32[2,2,4,1024]{3,2,1,0:T(4,128)S(1)}, u32[]{:S(2)}, u32[]{:S(2)}) collective-permute-start(f32[2,2,4,1024]{3,2,1,0:T(4,128)S(1)} %get-tuple-element.9), channel_id=1, source_target_pairs={{0,16},{8,24},{16,0},{24,8},{1,17},{9,25},{17,1},{25,9},{2,18},{10... | collective-permute-start | bytes 196616 | tf_op jit(solution)/shard_map/ppermute | solution.py:226
  45.4 0.7 collective-permute-done.3
  46.1 0.8 collective-permute-done.5
  46.9 1.3 %collective-permute-done.4 = f32[2,2,4,1024]{3,2,1,0:T(4,128)S(1)} collective-permute-done((f32[2,2,4,1024]{3,2,1,0:T(4,128)S(1)}, f32[2,2,4,1024]{3,2,1,0:T(4,128)S(1)}, u32[]{:S(2)}, u32[]{:S(2)}) %collective-permute-start.4) | collective-permute-done | bytes 65568 | tf_op jit(solution)/shard_map/ppermute | solution.py:226
  48.2 0.9 add_convert_fusion.2
  49.2 1.2 %collective-permute-done.6 = bf16[8,2,8,128]{3,2,1,0:T(8,128)(2,1)S(1)} collective-permute-done((bf16[8,2,8,128]{3,2,1,0:T(8,128)(2,1)S(1)}, bf16[8,2,8,128]{3,2,1,0:T(8,128)(2,1)S(1)}, u32[]{:S(2)}, u32[]{:S(2)}) %collective-permute-start.6) | collective-permute-done | bytes 32800 | tf_op jit(solution)/shard_map/ppermute | solution.py:172
  50.5 4.3 %collective-permute-done.7 = bf16[16,2,8,128]{3,2,1,0:T(8,128)(2,1)S(1)} collective-permute-done((bf16[16,2,8,128]{3,2,1,0:T(8,128)(2,1)S(1)}, bf16[16,2,8,128]{3,2,1,0:T(8,128)(2,1)S(1)}, u32[]{:S(2)}, u32[]{:S(2)}) %collective-permute-start.7) | collective-permute-done | bytes 65568 | tf_op jit(solution)/shard_map/ppermute | solution.py:172
  54.8 6.0 %collective-permute-done.8 = bf16[32,2,8,128]{3,2,1,0:T(8,128)(2,1)S(1)} collective-permute-done((bf16[32,2,8,128]{3,2,1,0:T(8,128)(2,1)S(1)}, bf16[32,2,8,128]{3,2,1,0:T(8,128)(2,1)S(1)}, u32[]{:S(2)}, u32[]{:S(2)}) %collective-permute-start.8) | collective-permute-done | bytes 131104 | tf_op jit(solution)/shard_map/ppermute | solution.py:172
  60.8 0.7 pad_maximum_fusion.1.g_ref
  61.5 16.9 %shard_map.60 = f32[8,2,4,1024]{3,2,1,0:T(4,128)} custom-call(s32[3136]{0:T(1024)} %reshape.203.aper_ref, s32[56]{0:T(128)} %get-tuple-element.17.blk_ref, s32[56]{0:T(128)} %get-tuple-element.16.chk_ref, s32[2]{0:T(128)} %pad_add_fusion.meta_ref, s32[8]{0:T(128)} %copy-done.2, bf16[2,2,8,49,128,128]{5,4,3,2,1,0:T(8,128)(2,1)} %resp_hbm.3, ...), custom_call_target="tpu_custom_call" | custom-call | tf_op jit(solution)/shard_map/pallas_call | solution.py:145
  78.4 0.9 %constant_dynamic-slice_fusion.2 = (f32[2,2,4,1024]{3,2,1,0:T(4,128)S(1)}, f32[2,2,4,1024]{3,2,1,0:T(4,128)S(1)}, f32[2,2,4,1024]{3,2,1,0:T(4,128)S(1)}) fusion(f32[8,2,4,1024]{3,2,1,0:T(4,128)} %shard_map.60, s32[]{:T(128)S(6)} %select_n.188, s32[]{:T(128)S(6)} %select_n.192, s32[]{:T(128)S(6)} %select_n.190), kind=kLoop, calls=%fused_computation.75 | loop fusion | bytes 393228 | tf_op jit(solution)/shard_map/dynamic_slice | solution.py:224
  79.3 1.3 %collective-permute-start.9 = (f32[2,2,4,1024]{3,2,1,0:T(4,128)S(1)}, f32[2,2,4,1024]{3,2,1,0:T(4,128)S(1)}, u32[]{:S(2)}, u32[]{:S(2)}) collective-permute-start(f32[2,2,4,1024]{3,2,1,0:T(4,128)S(1)} %get-tuple-element.4), channel_id=1, source_target_pairs={{0,8},{8,16},{16,24},{24,0},{1,9},{9,17},{17,25},{25,1},{2,10},{10... | collective-permute-start | bytes 196616 | tf_op jit(solution)/shard_map/ppermute | solution.py:226
  80.7 1.6 %collective-permute-start.11 = (f32[2,2,4,1024]{3,2,1,0:T(4,128)S(1)}, f32[2,2,4,1024]{3,2,1,0:T(4,128)S(1)}, u32[]{:S(2)}, u32[]{:S(2)}) collective-permute-start(f32[2,2,4,1024]{3,2,1,0:T(4,128)S(1)} %get-tuple-element.5), channel_id=1, source_target_pairs={{0,24},{8,0},{16,8},{24,16},{1,25},{9,1},{17,9},{25,17},{2,26},{10... | collective-permute-start | bytes 196616 | tf_op jit(solution)/shard_map/ppermute | solution.py:226
  82.3 1.5 %collective-permute-start.10 = (f32[2,2,4,1024]{3,2,1,0:T(4,128)S(1)}, f32[2,2,4,1024]{3,2,1,0:T(4,128)S(1)}, u32[]{:S(2)}, u32[]{:S(2)}) collective-permute-start(f32[2,2,4,1024]{3,2,1,0:T(4,128)S(1)} %get-tuple-element.6), channel_id=1, source_target_pairs={{0,16},{8,24},{16,0},{24,8},{1,17},{9,25},{17,1},{25,9},{2,18},{10... | collective-permute-start | bytes 196616 | tf_op jit(solution)/shard_map/ppermute | solution.py:226
  83.8 0.7 collective-permute-done.9
  84.5 0.8 collective-permute-done.11
  85.3 1.3 %collective-permute-done.10 = f32[2,2,4,1024]{3,2,1,0:T(4,128)S(1)} collective-permute-done((f32[2,2,4,1024]{3,2,1,0:T(4,128)S(1)}, f32[2,2,4,1024]{3,2,1,0:T(4,128)S(1)}, u32[]{:S(2)}, u32[]{:S(2)}) %collective-permute-start.10) | collective-permute-done | bytes 65568 | tf_op jit(solution)/shard_map/ppermute | solution.py:226
  86.6 1.5 %add_convert_fusion = bf16[2,2,4,1024]{3,2,1,0:T(4,128)(2,1)} fusion(bf16[2,2,4,1024]{3,2,1,0:T(4,128)(2,1)S(1)} %copy-done, f32[2,2,4,1024]{3,2,1,0:T(4,128)S(1)} %collective-permute-done.11, f32[2,2,4,1024]{3,2,1,0:T(4,128)S(1)} %collective-permute-done.10, f32[2,2,4,1024]{3,2,1,0:T(4,128)S(1)} %collective-permute-done.9, f32[8,2,4,1024]{3,2,1,0:T(4,128)} %shard_map.60, ...), kind=kLoop, calls=%fused_computation.49 | loop fusion | flops 131072 | bytes 327684 | tf_op jit(solution)/shard_map/convert_element_type | solution.py:247
  (34 shorter events, 2.4 us)
Async XLA Ops:
  1.4 5.4 %collective-permute-start = (bf16[8,2,8,128]{3,2,1,0:T(8,128)(2,1)S(1)}, bf16[8,2,8,128]{3,2,1,0:T(8,128)(2,1)S(1)}, u32[]{:S(2)}, u32[]{:S(2)}) collective-permute-start(bf16[8,2,8,128]{3,2,1,0:T(8,128)(2,1)S(1)} %bitcast.48), channel_id=1, source_target_pairs={{0,1},{1,0},{2,3},{3,2},{4,5},{5,4},{6,7},{7,6},{8,9},{9,8},{10,11... | collective-permute-start | bytes 98312 | tf_op jit(solution)/shard_map/ppermute | solution.py:172
  3.2 19.8 %copy-start.2 = (s32[8]{0:T(128)}, s32[8]{0:T(128)S(1)}, u32[]{:S(2)}) copy-start(s32[8]{0:T(128)S(1)} %convert_reduce_fusion.live_ref) | copy-start | bytes 100
  6.8 4.5 %collective-permute-start.1 = (bf16[16,2,8,128]{3,2,1,0:T(8,128)(2,1)S(1)}, bf16[16,2,8,128]{3,2,1,0:T(8,128)(2,1)S(1)}, u32[]{:S(2)}, u32[]{:S(2)}) collective-permute-start(bf16[16,2,8,128]{3,2,1,0:T(8,128)(2,1)S(1)} %pad_maximum_fusion.4), channel_id=1, source_target_pairs={{0,2},{1,3},{2,0},{3,1},{4,6},{5,7},{6,4},{7,5},{8,10},{9,11},{10,... | collective-permute-start | bytes 196616 | tf_op jit(solution)/shard_map/ppermute | solution.py:172
  11.4 11.0 %collective-permute-start.2 = (bf16[32,2,8,128]{3,2,1,0:T(8,128)(2,1)S(1)}, bf16[32,2,8,128]{3,2,1,0:T(8,128)(2,1)S(1)}, u32[]{:S(2)}, u32[]{:S(2)}) collective-permute-start(bf16[32,2,8,128]{3,2,1,0:T(8,128)(2,1)S(1)} %pad_maximum_fusion.2), channel_id=1, source_target_pairs={{0,4},{1,5},{2,6},{3,7},{4,0},{5,1},{6,2},{7,3},{8,12},{9,13},{10,... | collective-permute-start | bytes 393224 | tf_op jit(solution)/shard_map/ppermute | solution.py:172
  23.1 63.5 %copy-start = (bf16[2,2,4,1024]{3,2,1,0:T(4,128)(2,1)S(1)}, bf16[2,2,4,1024]{3,2,1,0:T(4,128)(2,1)}, u32[]{:S(2)}) copy-start(bf16[2,2,4,1024]{3,2,1,0:T(4,128)(2,1)} %param.6) | copy-start | bytes 98308
  40.9 5.2 %collective-permute-start.3 = (f32[2,2,4,1024]{3,2,1,0:T(4,128)S(1)}, f32[2,2,4,1024]{3,2,1,0:T(4,128)S(1)}, u32[]{:S(2)}, u32[]{:S(2)}) collective-permute-start(f32[2,2,4,1024]{3,2,1,0:T(4,128)S(1)} %get-tuple-element.7), channel_id=1, source_target_pairs={{0,8},{8,16},{16,24},{24,0},{1,9},{9,17},{17,25},{25,1},{2,10},{10... | collective-permute-start | bytes 196616 | tf_op jit(solution)/shard_map/ppermute | solution.py:226
  42.5 4.4 %collective-permute-start.5 = (f32[2,2,4,1024]{3,2,1,0:T(4,128)S(1)}, f32[2,2,4,1024]{3,2,1,0:T(4,128)S(1)}, u32[]{:S(2)}, u32[]{:S(2)}) collective-permute-start(f32[2,2,4,1024]{3,2,1,0:T(4,128)S(1)} %get-tuple-element.8), channel_id=1, source_target_pairs={{0,24},{8,0},{16,8},{24,16},{1,25},{9,1},{17,9},{25,17},{2,26},{10... | collective-permute-start | bytes 196616 | tf_op jit(solution)/shard_map/ppermute | solution.py:226
  43.9 4.3 %collective-permute-start.4 = (f32[2,2,4,1024]{3,2,1,0:T(4,128)S(1)}, f32[2,2,4,1024]{3,2,1,0:T(4,128)S(1)}, u32[]{:S(2)}, u32[]{:S(2)}) collective-permute-start(f32[2,2,4,1024]{3,2,1,0:T(4,128)S(1)} %get-tuple-element.9), channel_id=1, source_target_pairs={{0,16},{8,24},{16,0},{24,8},{1,17},{9,25},{17,1},{25,9},{2,18},{10... | collective-permute-start | bytes 196616 | tf_op jit(solution)/shard_map/ppermute | solution.py:226
  49.0 39.0 %copy-start.1 = (bf16[2,2,4,1024]{3,2,1,0:T(4,128)(2,1)}, bf16[2,2,4,1024]{3,2,1,0:T(4,128)(2,1)S(1)}, u32[]{:S(2)}) copy-start(bf16[2,2,4,1024]{3,2,1,0:T(4,128)(2,1)S(1)} %add_convert_fusion.2) | copy-start | bytes 98308
  49.1 1.3 %collective-permute-start.6 = (bf16[8,2,8,128]{3,2,1,0:T(8,128)(2,1)S(1)}, bf16[8,2,8,128]{3,2,1,0:T(8,128)(2,1)S(1)}, u32[]{:S(2)}, u32[]{:S(2)}) collective-permute-start(bf16[8,2,8,128]{3,2,1,0:T(8,128)(2,1)S(1)} %bitcast.52), channel_id=1, source_target_pairs={{0,1},{1,0},{2,3},{3,2},{4,5},{5,4},{6,7},{7,6},{8,9},{9,8},{10,11... | collective-permute-start | bytes 98312 | tf_op jit(solution)/shard_map/ppermute | solution.py:172
  50.4 4.3 %collective-permute-start.7 = (bf16[16,2,8,128]{3,2,1,0:T(8,128)(2,1)S(1)}, bf16[16,2,8,128]{3,2,1,0:T(8,128)(2,1)S(1)}, u32[]{:S(2)}, u32[]{:S(2)}) collective-permute-start(bf16[16,2,8,128]{3,2,1,0:T(8,128)(2,1)S(1)} %pad_maximum_fusion.5), channel_id=1, source_target_pairs={{0,2},{1,3},{2,0},{3,1},{4,6},{5,7},{6,4},{7,5},{8,10},{9,11},{10,... | collective-permute-start | bytes 196616 | tf_op jit(solution)/shard_map/ppermute | solution.py:172
  54.7 6.0 %collective-permute-start.8 = (bf16[32,2,8,128]{3,2,1,0:T(8,128)(2,1)S(1)}, bf16[32,2,8,128]{3,2,1,0:T(8,128)(2,1)S(1)}, u32[]{:S(2)}, u32[]{:S(2)}) collective-permute-start(bf16[32,2,8,128]{3,2,1,0:T(8,128)(2,1)S(1)} %pad_maximum_fusion.3), channel_id=1, source_target_pairs={{0,4},{1,5},{2,6},{3,7},{4,0},{5,1},{6,2},{7,3},{8,12},{9,13},{10,... | collective-permute-start | bytes 393224 | tf_op jit(solution)/shard_map/ppermute | solution.py:172
  79.3 5.2 %collective-permute-start.9 = (f32[2,2,4,1024]{3,2,1,0:T(4,128)S(1)}, f32[2,2,4,1024]{3,2,1,0:T(4,128)S(1)}, u32[]{:S(2)}, u32[]{:S(2)}) collective-permute-start(f32[2,2,4,1024]{3,2,1,0:T(4,128)S(1)} %get-tuple-element.4), channel_id=1, source_target_pairs={{0,8},{8,16},{16,24},{24,0},{1,9},{9,17},{17,25},{25,1},{2,10},{10... | collective-permute-start | bytes 196616 | tf_op jit(solution)/shard_map/ppermute | solution.py:226
  80.7 4.6 %collective-permute-start.11 = (f32[2,2,4,1024]{3,2,1,0:T(4,128)S(1)}, f32[2,2,4,1024]{3,2,1,0:T(4,128)S(1)}, u32[]{:S(2)}, u32[]{:S(2)}) collective-permute-start(f32[2,2,4,1024]{3,2,1,0:T(4,128)S(1)} %get-tuple-element.5), channel_id=1, source_target_pairs={{0,24},{8,0},{16,8},{24,16},{1,25},{9,1},{17,9},{25,17},{2,26},{10... | collective-permute-start | bytes 196616 | tf_op jit(solution)/shard_map/ppermute | solution.py:226
  82.3 4.3 %collective-permute-start.10 = (f32[2,2,4,1024]{3,2,1,0:T(4,128)S(1)}, f32[2,2,4,1024]{3,2,1,0:T(4,128)S(1)}, u32[]{:S(2)}, u32[]{:S(2)}) collective-permute-start(f32[2,2,4,1024]{3,2,1,0:T(4,128)S(1)} %get-tuple-element.6), channel_id=1, source_target_pairs={{0,16},{8,24},{16,0},{24,8},{1,17},{9,25},{17,1},{25,9},{2,18},{10... | collective-permute-start | bytes 196616 | tf_op jit(solution)/shard_map/ppermute | solution.py:226
